TPU v7x, 512 devices: a whole 4x4x16 slice. The times are simulated.
512 devices in a mesh: sub: 64 (over x, z), grp: 8 (over y, core).
Axes of the slice: x: 4, y: 4, z: 16, core: 2. Of those that a mesh axis runs over, the one named last changes fastest.
Arguments:
- tiles: bfloat16 [8, 4096, 128, 128], P('grp', 'sub'), may hold values from -6 to 6
- dest_owner: int32 [8, 4096], P('grp', 'sub'), may hold values from 0 to 63, as said below
- dest_slot: int32 [8, 4096], P('grp', 'sub'), may hold values from 0 to 7
- triples: int32 [3, 1024], replicated, may hold values from 130 to 4030, as said below
Outputs:
- bispectrum: float32 [512, 2, 1024], P('sub', None, 'grp')
Inputs may be any that keep to these rules, and one draw needn't show every extreme that they name: `dest_owner`: in each frame group, among the 64 tile frames of one index of sub, no owner is named more than 2 times; in each frame group one owner is named exactly 2 times by every index of sub. `triples`: each column holds the flat indices (a + 32) * 64 + (b + 32) of frequencies (a, b) = u, v and u + v.
All inputs are finite; a program needn't handle non-finite values.
Results may differ from a plain program's by a relative error of at most 0.012.
Values may be sent and summed in bfloat16 or wider, within the bound.
No kernel may reach another device: no remote copies, remote signals or barrier semaphores. Data moves between devices by JAX's collectives and lax.ppermute only.
A program may use at most 64 MiB of HBM per device.

v0:
```python
import math

import jax
import jax.numpy as jnp
from jax import lax
from jax.sharding import PartitionSpec as P

BOX = 64
OWN = 8


def make_tables(patch, box):
    rows = jnp.arange(patch, dtype=jnp.int32)[:, None]
    cols = jnp.arange(box, dtype=jnp.int32)[None, :] - box // 2 + patch
    phase = rows * cols % patch
    angle = 2.0 * math.pi * phase.astype(jnp.float32) / patch
    scale = 1.0 / math.sqrt(patch)
    cos_tab = (jnp.cos(angle) * scale).astype(jnp.bfloat16)
    sin_tab = (-jnp.sin(angle) * scale).astype(jnp.bfloat16)
    centre = (jnp.arange(patch, dtype=jnp.float32) + 0.5) / patch
    hann = 0.5 - 0.5 * jnp.cos(2.0 * math.pi * centre)
    window = hann[:, None] * hann[None, :]
    right = jnp.concatenate([cos_tab, sin_tab], axis=1)
    left = jnp.transpose(right)
    return (right, left, window)


def spectra_block(block, right, left, window):
    box = right.shape[1] // 2
    apodised = (block.astype(jnp.float32) * window).astype(jnp.bfloat16)
    half = jnp.einsum("nij,jc->nic", apodised, right, preferred_element_type=jnp.float32).astype(
        jnp.bfloat16
    )
    full = jnp.einsum("ki,nic->nkc", left, half, preferred_element_type=jnp.float32)
    real_part = full[:, :box, :box] - full[:, box:, box:]
    imag_part = full[:, :box, box:] + full[:, box:, :box]
    count = block.shape[0]
    return (
        jnp.stack([real_part, imag_part], axis=1).reshape(count, 2, box * box).astype(jnp.bfloat16)
    )


def spectra_all(frames, right, left, window):
    count = frames.shape[0]
    block_len = math.gcd(count, 32)
    shaped = frames.reshape(count // block_len, block_len, frames.shape[1], frames.shape[2])
    result = lax.map(lambda block: spectra_block(block, right, left, window), shaped)
    return result.reshape(count, 2, result.shape[-1])


def accumulate(spectrum, labels, triples):
    rows = spectrum.shape[0]
    freq = spectrum.shape[-1]
    flat = spectrum.reshape(rows * 2, freq)
    ntri = triples.shape[1]
    block_len = math.gcd(ntri, 256)
    tri_blocks = jnp.transpose(triples.reshape(3, ntri // block_len, block_len), (1, 0, 2))
    slot_ids = jnp.arange(OWN, dtype=jnp.float32)[:, None]
    onehot = (labels.astype(jnp.float32)[None, :] == slot_ids).astype(jnp.float32)
    freq_ids = jnp.arange(freq, dtype=jnp.int32)[:, None]

    def step(cols):
        picked = []
        for which in range(3):
            select = (freq_ids == cols[which][None, :]).astype(jnp.bfloat16)
            picked.append(
                jnp.dot(flat, select, preferred_element_type=jnp.float32).reshape(
                    rows, 2, block_len
                )
            )
        first, second, third = picked
        prod_real = first[:, 0] * second[:, 0] - first[:, 1] * second[:, 1]
        prod_imag = first[:, 0] * second[:, 1] + first[:, 1] * second[:, 0]
        out_real = prod_real * third[:, 0] + prod_imag * third[:, 1]
        out_imag = prod_imag * third[:, 0] - prod_real * third[:, 1]
        terms = jnp.stack([out_real, out_imag], axis=1)
        return jnp.einsum("kn,nct->kct", onehot, terms, precision=lax.Precision.HIGHEST)

    result = lax.map(step, tri_blocks)
    return jnp.transpose(result, (1, 2, 0, 3)).reshape(OWN, 2, ntri)


def local(tiles, dest_owner, dest_slot, triples):
    frames = tiles[0]
    owners = dest_owner[0]
    slots = dest_slot[0]
    count = frames.shape[0]
    patch = frames.shape[-1]
    peers = lax.axis_size("sub")
    capacity = 2 * count // peers
    right, left, window = make_tables(patch, BOX)
    owner_hot = (owners[:, None] == jnp.arange(peers, dtype=jnp.int32)[None, :]).astype(jnp.int32)
    before = jnp.cumsum(owner_hot, axis=0) - owner_hot
    rank = jnp.sum(before * owner_hot, axis=1)
    position = owners * capacity + rank
    match = (position[None, :] == jnp.arange(peers * capacity, dtype=jnp.int32)[:, None]).astype(
        jnp.int32
    )
    filled = jnp.sum(match, axis=1) > 0
    source = jnp.sum(match * jnp.arange(count, dtype=jnp.int32)[None, :], axis=1)
    labels = jnp.where(filled, slots[source], -1).astype(jnp.bfloat16).reshape(peers, capacity)
    picker = match.astype(jnp.bfloat16)
    flat_frames = frames.reshape(count, patch * patch)
    outgoing = jnp.dot(picker, flat_frames, preferred_element_type=jnp.float32).astype(jnp.bfloat16)
    outgoing = outgoing.reshape(peers, capacity, patch, patch)
    received = lax.all_to_all(outgoing, "sub", split_axis=0, concat_axis=0, tiled=True)
    marks = lax.all_to_all(labels, "sub", split_axis=0, concat_axis=0, tiled=True)
    lead = received.shape[0]
    items = received.shape[1]
    flat = spectra_all(received.reshape(lead * items, patch, patch), right, left, window)
    spectrum = flat.reshape(lead, items, 2, flat.shape[-1])
    arrived = marks
    spectrum = spectrum.reshape(peers * capacity, 2, spectrum.shape[-1])
    arrived = arrived.reshape(peers * capacity)
    partial_value = accumulate(spectrum, arrived, triples)
    return lax.psum_scatter(partial_value, "grp", scatter_dimension=2, tiled=True)


def solution(mesh):
    in_specs = (P("grp", "sub", None, None), P("grp", "sub"), P("grp", "sub"), P())
    out_specs = P("sub", None, "grp")
    return jax.shard_map(local, mesh=mesh, in_specs=in_specs, out_specs=out_specs, check_vma=False)
```

profile of v0, /device:TPU:6, one launch (start us, length us, event | category | flops | bytes accessed | tf_op | source)
XLA Modules:
  0.0 333.1 jit_solution(12523955900139614967)
XLA Ops:
  9.0 1.2 gather_fusion
  11.0 18.8 %all-to-all-start.1 = ((bf16[64,1,2]{2,1,0:T(2,128)(2,1)}), bf16[64,1,2]{2,1,0:T(2,128)(2,1)S(1)}, u32[]{:S(2)}, u32[]{:S(2)}) async-start(bf16[64,1,2]{2,1,0:T(2,128)(2,1)} %convert_element_type.94), calls=%async_computation.1 | async-start | bytes 65536 | tf_op jit(solution)/shard_map/all_to_all | solution.py:107
  29.8 3.3 fusion.39
  33.1 3.2 copy.64
  36.3 6.0 %all-to-all-done.1 = bf16[64,1,2]{2,1,0:T(2,128)(2,1)S(1)} async-done(((bf16[64,1,2]{2,1,0:T(2,128)(2,1)}), bf16[64,1,2]{2,1,0:T(2,128)(2,1)S(1)}, u32[]{:S(2)}, u32[]{:S(2)}) %all-to-all-start.1) | async-done | bytes 288 | tf_op jit(solution)/shard_map/all_to_all | solution.py:107
  42.3 9.3 %all-to-all-start = ((bf16[64,2,128,128]{3,2,1,0:T(8,128)(2,1)}), bf16[64,2,128,128]{3,2,1,0:T(8,128)(2,1)}, u32[]{:S(2)}, u32[]{:S(2)}) async-start(bf16[64,2,128,128]{3,2,1,0:T(8,128)(2,1)} %bitcast.100), calls=%async_computation | async-start | bytes 8388608 | tf_op jit(solution)/shard_map/all_to_all | solution.py:106
  52.6 184.4 %all-to-all-done = bf16[64,2,128,128]{3,2,1,0:T(8,128)(2,1)} async-done(((bf16[64,2,128,128]{3,2,1,0:T(8,128)(2,1)}), bf16[64,2,128,128]{3,2,1,0:T(8,128)(2,1)}, u32[]{:S(2)}, u32[]{:S(2)}) %all-to-all-start) | async-done | bytes 4194336 | tf_op jit(solution)/shard_map/all_to_all | solution.py:106
  237.0 23.0 %while.23 = (s32[]{:T(128)}, bf16[4,32,2,4096]{3,2,1,0:T(2,128)(2,1)}, bf16[4,32,128,128]{3,2,1,0:T(8,128)(2,1)}, bf16[128,128]{1,0:T(8,128)(2,1)S(1)}, bf16[128...) while((s32[]{:T(128)}, bf16[4,32,2,4096]{3,2,1,0:T(2,128)(2,1)}, ...), condition=%wide.region_3.4_spmd.clone, body=%wide.region_2.3_spmd.clone.sunk | while | flops 271335424 | bytes 10159693 | solution.py:47
  237.1 2.1 convolution_bitcast_fusion.3
  241.4 1.4 copy_dynamic-update-slice_fusion.2
  242.8 2.1 convolution_bitcast_fusion.3
  247.1 1.4 copy_dynamic-update-slice_fusion.2
  248.6 2.1 convolution_bitcast_fusion.3
  252.9 1.4 copy_dynamic-update-slice_fusion.2
  254.4 2.1 convolution_bitcast_fusion.3
  258.7 1.3 copy_dynamic-update-slice_fusion.2
  260.0 2.7 reshape_reshape_reshape_reshape.3
  262.7 21.1 %while.24 = (s32[]{:T(128)}, f32[4,8,2,256]{3,1,2,0:T(8,128)S(1)}, s32[4,3,256]{2,1,0:T(4,128)}, bf16[256,4096]{1,0:T(8,128)(2,1)S(1)}, f32[128]{0:T(128)S(1)}, /*index=5*/s32[]{:T(128)}, s32[]{:T(128)}, s32[]{}, s32[]{}) while((s32[]{:T(128)}, f32[4,8,2,256]{3,1,2,0:T(8,128)S(1)}, s32[4,3,256]{2,1,0:T(4,128)}, ...), condition=%wide.region_7.8_spmd.clone.clone, body=%wide.region_6.7_spmd.clone.clone.sunk | while | flops 1620510720 | bytes 12347013 | solution.py:79
  270.0 1.0 fusion.87
  275.3 1.0 fusion.87
  283.8 2.6 copy.53
  286.5 3.9 %reshape.167 = f32[1024,16]{1,0:T(8,128)} reshape(f32[1024,8,2]{2,1,0:T(8,128)} %bitcast.101) | data formatting | bytes 131072
  290.4 34.0 %reduce-scatter.4.cloned.1.call-done = f32[128,16]{1,0:T(8,128)} async-done(((f32[1024,16]{1,0:T(8,128)}), f32[128,16]{1,0:T(8,128)}) %reduce-scatter.4.cloned.1.call-update) | async-done | bytes 8208
  324.4 1.0 reshape.168
  (97 shorter events, 32.8 us)
Async XLA Ops:
  6.5 2.5 copy-start
  11.0 31.3 %all-to-all-start.1 = ((bf16[64,1,2]{2,1,0:T(2,128)(2,1)}), bf16[64,1,2]{2,1,0:T(2,128)(2,1)S(1)}, u32[]{:S(2)}, u32[]{:S(2)}) async-start(bf16[64,1,2]{2,1,0:T(2,128)(2,1)} %convert_element_type.94), calls=%async_computation.1 | async-start | bytes 65536 | tf_op jit(solution)/shard_map/all_to_all | solution.py:107
  42.3 194.6 %all-to-all-start = ((bf16[64,2,128,128]{3,2,1,0:T(8,128)(2,1)}), bf16[64,2,128,128]{3,2,1,0:T(8,128)(2,1)}, u32[]{:S(2)}, u32[]{:S(2)}) async-start(bf16[64,2,128,128]{3,2,1,0:T(8,128)(2,1)} %bitcast.100), calls=%async_computation | async-start | bytes 8388608 | tf_op jit(solution)/shard_map/all_to_all | solution.py:106
  51.7 272.7 %reduce-scatter.4.cloned.1.call-start = ((), (), s32[]{:S(2)}) async-start(), calls=%async_computation.3 | async-start | bytes 589824
Sparse Core Ops, SparseCore 0:
  290.6 33.8 reduce-scatter.3
where the time goes:
time: 334 us; the launch traced here: 333 us
  waiting for transfers between devices  224 us (67%)
  local copies, waits for them, and re-layouts  35.6 us (11%)
  starting transfers between devices  28.3 us (8%)
  matrix products  24.5 us (7%)
  between operations  13.5 us (4%)
  other arithmetic  6.25 us (2%)
    all_to_all x1, waiting for transfers between devices, local(): lax.all_to_all(outgoing, 'sub', split_axis=0, concat_axis=0, tiled=True)  184 us
    unnamed x2, waiting for transfers between devices  34 us
    all_to_all x1, starting transfers between devices, local(): lax.all_to_all(labels, 'sub', split_axis=0, concat_axis=0, tiled=True)  18.8 us
    dot_general x12, matrix products, step(): jnp.dot(flat, select, preferred_element_type=jnp.float32)  11.9 us
    unnamed x8, local copies, waits for them, and re-layouts  11.7 us
    all_to_all x1, starting transfers between devices, local(): lax.all_to_all(outgoing, 'sub', split_axis=0, concat_axis=0, tiled=True)  9.32 us
    dot_general x4, matrix products, spectra_block(): jnp.einsum('ki,nic->nkc', left, half, preferred_element_type=jnp.float32)  8.32 us
  transfers between devices with their start and end apart: 3, of which 3 were waited for; matrix products, arithmetic and copies ran while one was open for 2% of the time, Pallas kernels for 0%

commit v1 on v0

v1 whole, which is shorter than its diff:
```python
import math

import jax
import jax.numpy as jnp
from jax import lax
from jax.sharding import PartitionSpec as P

BOX = 64
OWN = 8


def make_tables(patch, box):
    rows = jnp.arange(patch, dtype=jnp.int32)[:, None]
    cols = jnp.arange(box, dtype=jnp.int32)[None, :] - box // 2 + patch
    phase = rows * cols % patch
    angle = 2.0 * math.pi * phase.astype(jnp.float32) / patch
    scale = 1.0 / math.sqrt(patch)
    cos_tab = (jnp.cos(angle) * scale).astype(jnp.bfloat16)
    sin_tab = (-jnp.sin(angle) * scale).astype(jnp.bfloat16)
    centre = (jnp.arange(patch, dtype=jnp.float32) + 0.5) / patch
    hann = 0.5 - 0.5 * jnp.cos(2.0 * math.pi * centre)
    window = hann[:, None] * hann[None, :]
    right = jnp.concatenate([cos_tab, sin_tab], axis=1)
    left = jnp.transpose(right)
    return (right, left, window)


def spectra_freq_major(frames, right, left, window):
    box = right.shape[1] // 2
    count = frames.shape[0]
    apodised = (frames.astype(jnp.float32) * window).astype(jnp.bfloat16)
    half = jnp.einsum("nij,jc->nic", apodised, right, preferred_element_type=jnp.float32).astype(
        jnp.bfloat16
    )
    full = jnp.einsum("ki,nic->kcn", left, half, preferred_element_type=jnp.float32)
    real_part = full[:box, :box] - full[box:, box:]
    imag_part = full[:box, box:] + full[box:, :box]
    spec = jnp.stack([real_part, imag_part], axis=2).astype(jnp.bfloat16)
    return spec.reshape(box * box, 2 * count)


def local(tiles, dest_owner, dest_slot, triples):
    frames = tiles[0]
    count = frames.shape[0]
    patch = frames.shape[-1]
    groups = lax.axis_size("grp")
    peers = lax.axis_size("sub")
    target = dest_owner[0] * OWN + dest_slot[0]
    right, left, window = make_tables(patch, BOX)
    spec = spectra_freq_major(frames, right, left, window)
    picked = [jnp.take(spec, triples[w], axis=0).astype(jnp.float32) for w in range(3)]
    ntri = triples.shape[1]
    first, second, third = [p.reshape(ntri, 2, count) for p in picked]
    prod_real = first[:, 0] * second[:, 0] - first[:, 1] * second[:, 1]
    prod_imag = first[:, 0] * second[:, 1] + first[:, 1] * second[:, 0]
    out_real = prod_real * third[:, 0] + prod_imag * third[:, 1]
    out_imag = prod_imag * third[:, 0] - prod_real * third[:, 1]
    terms = jnp.stack([out_real, out_imag], axis=1)
    block = ntri // groups
    terms = terms.reshape(groups, block, 2, count)
    marks = jnp.broadcast_to(target.astype(jnp.float32)[None, None, None, :], (groups, 8, 2, count))
    payload = jnp.concatenate([terms, marks], axis=1)
    got = lax.all_to_all(payload, "grp", split_axis=0, concat_axis=0, tiled=True)
    got_terms = got[:, :block]
    got_marks = got[:, block, 0, :].astype(jnp.int32)
    rows = peers * OWN
    onehot = (
        got_marks[None, :, :] == jnp.arange(rows, dtype=jnp.int32)[:, None, None]
    ).astype(jnp.float32)
    partial_value = jnp.einsum(
        "rgn,gtcn->rct", onehot, got_terms, precision=lax.Precision.HIGHEST
    )
    return lax.psum_scatter(partial_value, "sub", scatter_dimension=0, tiled=True)


def solution(mesh):
    in_specs = (P("grp", "sub", None, None), P("grp", "sub"), P("grp", "sub"), P())
    out_specs = P("sub", None, "grp")
    return jax.shard_map(local, mesh=mesh, in_specs=in_specs, out_specs=out_specs, check_vma=False)
```

time: 334 us -> 338 us (1.012)
  waiting for transfers between devices: 224 us -> 265 us
  starting transfers between devices: 28.3 us -> 0.01 us
  blocking collectives: 0 us -> 20.4 us
  matrix products: 24.5 us -> 5.75 us
  local copies, waits for them, and re-layouts: 35.6 us -> 24.5 us
    unnamed x2, waiting for transfers between devices: 34 us -> 265 us
    all_to_all x2 -> x0, waiting for transfers between devices: 190 us -> none  [the longest x1 184 us: local(): lax.all_to_all(outgoing, 'sub', split_axis=0, concat_axis=0, tiled=True)]
    all_to_all x2 -> x0, starting transfers between devices: 28.1 us -> none  [the longest x1 18.8 us: local(): lax.all_to_all(labels, 'sub', split_axis=0, concat_axis=0, tiled=True)]
    all_to_all x0 -> x1, blocking collectives: none -> 20.4 us  [local(): lax.all_to_all(payload, 'grp', split_axis=0, concat_axis=0, tiled=True)]
    dot_general x21 -> x2, matrix products: 24.5 us -> 5.75 us  [the longest x1 4.96 us: spectra_freq_major(): jnp.einsum('ki,nic->kcn', left, half, preferred_element_type=jnp.float32)]
    another operation x17 -> x0, local copies, waits for them, and re-layouts: 8.8 us -> none  [the longest x8 3.72 us: spectra_block(): jnp.stack([real_part, imag_part], axis=1).reshape(count, 2, box * box)]
    unnamed x8 -> x9, local copies, waits for them, and re-layouts: 11.7 us -> 3.13 us
    gather x1 -> x3, local copies, waits for them, and re-layouts: 1.23 us -> 9.62 us  [local(): jnp.take(spec, triples[w], axis=0).astype(jnp.float32)]
  transfers between devices with their start and end apart: 3 -> 1, of which waited for: 3 -> 1; matrix products, arithmetic and copies ran while one was open for 2% -> 0% of each run, Pallas kernels for 0% -> 0%
where the time goes in v1:
time: 338 us; the launch traced here: 336 us
  waiting for transfers between devices  265 us (78%)
  local copies, waits for them, and re-layouts  24.5 us (7%)
  blocking collectives  20.4 us (6%)
  between operations  14.3 us (4%)
  other arithmetic  6.42 us (2%)
  matrix products  5.75 us (2%)
    unnamed x2, waiting for transfers between devices  265 us
    all_to_all x1, blocking collectives, local(): lax.all_to_all(payload, 'grp', split_axis=0, concat_axis=0, tiled=True)  20.4 us
    gather x3, local copies, waits for them, and re-layouts, local(): jnp.take(spec, triples[w], axis=0).astype(jnp.float32)  9.62 us
    convert_element_type x2, local copies, waits for them, and re-layouts, spectra_freq_major(): spec = jnp.stack([real_part, imag_part], axis=2).astype(jnp.bfloat16)  8.56 us
  transfers between devices with their start and end apart: 1, of which 1 were waited for; matrix products, arithmetic and copies ran while one was open for 0% of the time, Pallas kernels for 0%

profile of v1, /device:TPU:6, one launch (start us, length us, event | category | flops | bytes accessed | tf_op | source)
XLA Modules:
  0.0 336.1 jit_solution(12006324887587864392)
XLA Ops:
  6.6 0.8 fusion.34
  7.5 0.2 multiply_convert_fusion.1
  7.8 5.0 %convolution_bitcast_fusion = f32[128,128,64]{0,1,2:T(8,128)} fusion(bf16[1,64,128,128]{3,2,1,0:T(8,128)(2,1)} %param.6, f32[128,128]{1,0:T(8,128)S(1)} %broadcast_multiply_fusion, bf16[128,64]{0,1:T(8,128)(2,1)S(1)} %get-tuple-element.15, bf16[128,64]{0,1:T(8,128)(2,1)S(1)} %get-tuple-element.14), kind=kOutput, calls=%fused_computation.5 | convolution fusion | flops 541196288 | bytes 6389760 | tf_op jit(solution)/shard_map/ki,nic->kcn/dot_general | solution.py:35
  12.8 4.7 %fusion.13 = (bf16[64,64,1,64]{0,1,3,2:T(8,128)(2,1)S(1)}, bf16[64,64,1,64]{0,1,3,2:T(8,128)(2,1)S(1)}) fusion(f32[128,128,64]{0,1,2:T(8,128)} %convolution_bitcast_fusion), kind=kLoop, calls=%fused_computation.16 | loop fusion | flops 1048576 | bytes 5242880 | tf_op jit(solution)/shard_map/stack | solution.py:38
  17.5 0.5 pad_maximum_fusion
  17.9 4.7 %copy.48 = bf16[64,64,2,64]{3,2,1,0:T(2,128)(2,1)} copy(bf16[64,64,2,64]{0,1,3,2:T(8,128)(2,1)S(1)} %pad_maximum_fusion) | data formatting | bytes 2097152 | tf_op jit(solution)/shard_map/convert_element_type | solution.py:38
  22.6 3.9 %reshape.152 = bf16[4096,128]{1,0:T(8,128)(2,1)S(1)} reshape(bf16[64,64,2,64]{3,2,1,0:T(2,128)(2,1)} %copy.48) | data formatting | bytes 2097152 | tf_op jit(solution)/shard_map/convert_element_type | solution.py:38
  26.5 3.2 gather_fusion.2
  29.7 0.2 select_convert_fusion
  29.9 0.2 copy.37
  30.1 3.2 gather_fusion
  33.3 0.2 select_convert_fusion.2
  33.6 0.2 copy.33
  33.8 3.2 gather_fusion.1
  37.0 0.2 select_convert_fusion.1
  37.2 0.2 copy.35
  37.7 0.3 copy-done
  38.3 0.6 copy.38
  38.9 20.4 %all_to_all.5 = f32[8,136,2,64]{1,3,2,0:T(8,128)S(1)} all-to-all(f32[8,136,2,64]{1,3,2,0:T(8,128)S(1)} %copy.38), channel_id=1, replica_groups=mesh['sub'=64,'grp'=8] {'grp'}, dimensions={0} | all-to-all | bytes 1114112 | tf_op jit(solution)/shard_map/all_to_all | solution.py:63
  59.4 0.8 convolution_bitcast_fusion.1
  60.2 1.0 copy.41
  61.3 1.3 dynamic-slice
  63.2 264.7 %all-reduce.3.cloned.1.call-done = f32[512,2,128]{2,1,0:T(2,128)} async-done(((f32[512,2,128]{2,1,0:T(2,128)}), f32[512,2,128]{2,1,0:T(2,128)}) %all-reduce.3.cloned.1.call-update) | async-done | bytes 524304
  327.9 1.3 constant_dynamic-slice_fusion
  (24 shorter events, 0.9 us)
Async XLA Ops:
  6.5 321.4 %all-reduce.3.cloned.1.call-start = ((), (), s32[]{:S(2)}) async-start(), calls=%async_computation.1 | async-start | bytes 1048576
  37.4 0.7 copy-start
  37.4 0.7 copy-start.1
Sparse Core Ops, SparseCore 0:
  61.4 266.4 all-reduce.2

commit v2 on v1

--- a/solution.py
+++ b/solution.py
@@ -70,7 +70,9 @@
     partial_value = jnp.einsum(
         "rgn,gtcn->rct", onehot, got_terms, precision=lax.Precision.HIGHEST
     )
-    return lax.psum_scatter(partial_value, "sub", scatter_dimension=0, tiled=True)
+    shaped = partial_value.reshape(peers, OWN, 2, block)
+    gathered = lax.all_to_all(shaped, "sub", split_axis=0, concat_axis=0, tiled=True)
+    return jnp.sum(gathered, axis=0)
 
 
 def solution(mesh):

time: 338 us -> 104 us (0.31)
  waiting for transfers between devices: 265 us -> 0 us
  blocking collectives: 20.4 us -> 69.7 us
  between operations: 14.3 us -> 0.25 us
    unnamed x2 -> x0, waiting for transfers between devices: 265 us -> none
    all_to_all x0 -> x1, blocking collectives: none -> 49.4 us  [local(): lax.all_to_all(shaped, 'sub', split_axis=0, concat_axis=0, tiled=True)]
  transfers between devices with their start and end apart: 1 -> 0, of which waited for: 1 -> 0; matrix products, arithmetic and copies ran while one was open for 0% -> 0% of each run, Pallas kernels for 0% -> 0%
where the time goes in v2:
time: 104 us
  blocking collectives  69.7 us (67%)
  local copies, waits for them, and re-layouts  21.8 us (21%)
  other arithmetic  6.49 us (6%)
  matrix products  5.74 us (6%)
    all_to_all x1, blocking collectives, local(): lax.all_to_all(shaped, 'sub', split_axis=0, concat_axis=0, tiled=True)  49.4 us
    all_to_all x1, blocking collectives, local(): lax.all_to_all(payload, 'grp', split_axis=0, concat_axis=0, tiled=True)  20.4 us
    gather x3, local copies, waits for them, and re-layouts, local(): jnp.take(spec, triples[w], axis=0).astype(jnp.float32)  9.63 us
    convert_element_type x2, local copies, waits for them, and re-layouts, spectra_freq_major(): spec = jnp.stack([real_part, imag_part], axis=2).astype(jnp.bfloat16)  8.56 us
    another operation x2, other arithmetic, spectra_freq_major(): spec = jnp.stack([real_part, imag_part], axis=2).astype(jnp.bfloat16)  5.13 us
    dot_general x1, matrix products, spectra_freq_major(): jnp.einsum('ki,nic->kcn', left, half, preferred_element_type=jnp.float32)  4.95 us

profile of v2, /device:TPU:6, one launch (start us, length us, event | category | flops | bytes accessed | tf_op | source)
XLA Modules:
  0.0 104.0 jit_solution(2803336756092041390)
XLA Ops:
  0.1 0.8 fusion.34
  1.0 0.2 multiply_convert_fusion.1
  1.3 5.0 %convolution_bitcast_fusion = f32[128,128,64]{0,1,2:T(8,128)} fusion(bf16[1,64,128,128]{3,2,1,0:T(8,128)(2,1)} %param.6, f32[128,128]{1,0:T(8,128)S(1)} %broadcast_multiply_fusion, bf16[128,64]{0,1:T(8,128)(2,1)S(1)} %get-tuple-element.15, bf16[128,64]{0,1:T(8,128)(2,1)S(1)} %get-tuple-element.14), kind=kOutput, calls=%fused_computation.5 | convolution fusion | flops 541196288 | bytes 6389760 | tf_op jit(solution)/shard_map/ki,nic->kcn/dot_general | solution.py:35
  6.2 4.7 %fusion.13 = (bf16[64,64,1,64]{0,1,3,2:T(8,128)(2,1)S(1)}, bf16[64,64,1,64]{0,1,3,2:T(8,128)(2,1)S(1)}) fusion(f32[128,128,64]{0,1,2:T(8,128)} %convolution_bitcast_fusion), kind=kLoop, calls=%fused_computation.16 | loop fusion | flops 1048576 | bytes 5242880 | tf_op jit(solution)/shard_map/stack | solution.py:38
  10.9 0.5 pad_maximum_fusion
  11.4 4.7 %copy.53 = bf16[64,64,2,64]{3,2,1,0:T(2,128)(2,1)} copy(bf16[64,64,2,64]{0,1,3,2:T(8,128)(2,1)S(1)} %pad_maximum_fusion) | data formatting | bytes 2097152 | tf_op jit(solution)/shard_map/convert_element_type | solution.py:38
  16.1 3.9 %reshape.155 = bf16[4096,128]{1,0:T(8,128)(2,1)S(1)} reshape(bf16[64,64,2,64]{3,2,1,0:T(2,128)(2,1)} %copy.53) | data formatting | bytes 2097152 | tf_op jit(solution)/shard_map/convert_element_type | solution.py:38
  20.0 3.2 %gather_fusion.2 = bf16[1024,128]{1,0:T(8,128)(2,1)S(1)} fusion(bf16[4096,128]{1,0:T(8,128)(2,1)S(1)} %reshape.155, s32[1024]{0:T(1024)S(1)} %fusion.31), kind=kCustom, calls=%fused_computation.2.clone | custom fusion | bytes 528384 | tf_op jit(solution)/shard_map/jit(_take)/gather | solution.py:51
  23.2 0.2 select_convert_fusion
  23.4 0.2 copy.39
  23.6 3.2 %gather_fusion = bf16[1024,128]{1,0:T(8,128)(2,1)S(1)} fusion(bf16[4096,128]{1,0:T(8,128)(2,1)S(1)} %reshape.155, s32[1024]{0:T(1024)S(1)} %fusion.29), kind=kCustom, calls=%fused_computation.clone | custom fusion | bytes 528384 | tf_op jit(solution)/shard_map/jit(_take)/gather | solution.py:51
  26.8 0.2 select_convert_fusion.2
  27.0 0.2 copy.35
  27.2 3.2 %gather_fusion.1 = bf16[1024,128]{1,0:T(8,128)(2,1)S(1)} fusion(bf16[4096,128]{1,0:T(8,128)(2,1)S(1)} %reshape.155, s32[1024]{0:T(1024)S(1)} %fusion.30), kind=kCustom, calls=%fused_computation.1.clone | custom fusion | bytes 528384 | tf_op jit(solution)/shard_map/jit(_take)/gather | solution.py:51
  30.4 0.2 select_convert_fusion.1
  30.6 0.2 copy.37
  30.9 0.1 add_bitcast_fusion
  31.2 0.3 copy-done
  31.8 0.6 copy.40
  32.4 20.4 %all_to_all.10 = f32[8,136,2,64]{1,3,2,0:T(8,128)S(1)} all-to-all(f32[8,136,2,64]{1,3,2,0:T(8,128)S(1)} %copy.40), channel_id=1, replica_groups=mesh['sub'=64,'grp'=8] {'grp'}, dimensions={0} | all-to-all | bytes 1114112 | tf_op jit(solution)/shard_map/all_to_all | solution.py:63
  52.9 0.8 convolution_bitcast_fusion.1
  53.7 0.2 copy.43
  53.9 49.4 %all_to_all.11 = f32[64,8,2,128]{3,1,2,0:T(8,128)S(1)} all-to-all(f32[64,8,2,128]{3,1,2,0:T(8,128)S(1)} %copy.44), channel_id=1, replica_groups=mesh['sub'=64,'grp'=8] {'sub'}, dimensions={0} | all-to-all | bytes 1048576 | tf_op jit(solution)/shard_map/all_to_all | solution.py:74
  103.4 0.6 copy.46
  (23 shorter events, 0.8 us)
Async XLA Ops:
  30.9 0.7 copy-start
  30.9 0.7 copy-start.1

commit v3 on v2

--- a/solution.py
+++ b/solution.py
@@ -55,24 +55,26 @@
     prod_imag = first[:, 0] * second[:, 1] + first[:, 1] * second[:, 0]
     out_real = prod_real * third[:, 0] + prod_imag * third[:, 1]
     out_imag = prod_imag * third[:, 0] - prod_real * third[:, 1]
-    terms = jnp.stack([out_real, out_imag], axis=1)
+    terms = jnp.stack([out_real, out_imag], axis=1).astype(jnp.bfloat16)
     block = ntri // groups
     terms = terms.reshape(groups, block, 2, count)
-    marks = jnp.broadcast_to(target.astype(jnp.float32)[None, None, None, :], (groups, 8, 2, count))
+    label = jnp.stack([dest_owner[0], dest_slot[0]]).astype(jnp.bfloat16)
+    marks = jnp.broadcast_to(label[None, None, :, :], (groups, 16, 2, count))
     payload = jnp.concatenate([terms, marks], axis=1)
     got = lax.all_to_all(payload, "grp", split_axis=0, concat_axis=0, tiled=True)
     got_terms = got[:, :block]
-    got_marks = got[:, block, 0, :].astype(jnp.int32)
+    got_label = got[:, block].astype(jnp.int32)
+    got_marks = got_label[:, 0, :] * OWN + got_label[:, 1, :]
     rows = peers * OWN
     onehot = (
         got_marks[None, :, :] == jnp.arange(rows, dtype=jnp.int32)[:, None, None]
-    ).astype(jnp.float32)
+    ).astype(jnp.bfloat16)
     partial_value = jnp.einsum(
-        "rgn,gtcn->rct", onehot, got_terms, precision=lax.Precision.HIGHEST
+        "rgn,gtcn->rct", onehot, got_terms, preferred_element_type=jnp.float32
     )
-    shaped = partial_value.reshape(peers, OWN, 2, block)
+    shaped = partial_value.astype(jnp.bfloat16).reshape(peers, OWN, 2, block)
     gathered = lax.all_to_all(shaped, "sub", split_axis=0, concat_axis=0, tiled=True)
-    return jnp.sum(gathered, axis=0)
+    return jnp.sum(gathered.astype(jnp.float32), axis=0)
 
 
 def solution(mesh):

time: 104 us -> 87.7 us (0.84)
  blocking collectives: 69.7 us -> 53.8 us
    all_to_all x1, blocking collectives: 49.4 us -> 39.1 us  [local(): lax.all_to_all(shaped, 'sub', split_axis=0, concat_axis=0, tiled=True)]
    all_to_all x1, blocking collectives: 20.4 us -> 14.7 us  [local(): lax.all_to_all(payload, 'grp', split_axis=0, concat_axis=0, tiled=True)]
where the time goes in v3:
time: 87.7 us; the launch traced here: 87.4 us
  blocking collectives  53.8 us (61%)
  local copies, waits for them, and re-layouts  21.4 us (24%)
  other arithmetic  6.55 us (7%)
  matrix products  5.42 us (6%)
    all_to_all x1, blocking collectives, local(): lax.all_to_all(shaped, 'sub', split_axis=0, concat_axis=0, tiled=True)  39.1 us
    all_to_all x1, blocking collectives, local(): lax.all_to_all(payload, 'grp', split_axis=0, concat_axis=0, tiled=True)  14.7 us
    gather x3, local copies, waits for them, and re-layouts, local(): jnp.take(spec, triples[w], axis=0).astype(jnp.float32)  9.62 us
    convert_element_type x2, local copies, waits for them, and re-layouts, spectra_freq_major(): spec = jnp.stack([real_part, imag_part], axis=2).astype(jnp.bfloat16)  8.56 us
    another operation x2, other arithmetic, spectra_freq_major(): spec = jnp.stack([real_part, imag_part], axis=2).astype(jnp.bfloat16)  5.13 us
    dot_general x1, matrix products, spectra_freq_major(): jnp.einsum('ki,nic->kcn', left, half, preferred_element_type=jnp.float32)  4.95 us

profile of v3, /device:TPU:6, one launch (start us, length us, event | category | flops | bytes accessed | tf_op | source)
XLA Modules:
  0.0 87.4 jit_solution(40478034933476941)
XLA Ops:
  0.1 0.8 fusion.39
  1.0 0.2 multiply_convert_fusion.1
  1.3 5.0 %convolution_bitcast_fusion = f32[128,128,64]{0,1,2:T(8,128)} fusion(bf16[1,64,128,128]{3,2,1,0:T(8,128)(2,1)} %param.6, f32[128,128]{1,0:T(8,128)S(1)} %broadcast_multiply_fusion, bf16[128,64]{0,1:T(8,128)(2,1)S(1)} %get-tuple-element.15, bf16[128,64]{0,1:T(8,128)(2,1)S(1)} %get-tuple-element.14), kind=kOutput, calls=%fused_computation.5 | convolution fusion | flops 541196288 | bytes 6389760 | tf_op jit(solution)/shard_map/ki,nic->kcn/dot_general | solution.py:35
  6.2 4.7 %fusion.15 = (bf16[64,64,1,64]{0,1,3,2:T(8,128)(2,1)S(1)}, bf16[64,64,1,64]{0,1,3,2:T(8,128)(2,1)S(1)}) fusion(f32[128,128,64]{0,1,2:T(8,128)} %convolution_bitcast_fusion), kind=kLoop, calls=%fused_computation.18 | loop fusion | flops 1048576 | bytes 5242880 | tf_op jit(solution)/shard_map/stack | solution.py:38
  10.9 0.5 pad_maximum_fusion
  11.4 4.7 %copy.53 = bf16[64,64,2,64]{3,2,1,0:T(2,128)(2,1)} copy(bf16[64,64,2,64]{0,1,3,2:T(8,128)(2,1)S(1)} %pad_maximum_fusion) | data formatting | bytes 2097152 | tf_op jit(solution)/shard_map/convert_element_type | solution.py:38
  16.1 3.9 %reshape.167 = bf16[4096,128]{1,0:T(8,128)(2,1)S(1)} reshape(bf16[64,64,2,64]{3,2,1,0:T(2,128)(2,1)} %copy.53) | data formatting | bytes 2097152 | tf_op jit(solution)/shard_map/convert_element_type | solution.py:38
  20.0 3.2 %gather_fusion.2 = bf16[1024,128]{1,0:T(8,128)(2,1)S(1)} fusion(bf16[4096,128]{1,0:T(8,128)(2,1)S(1)} %reshape.167, s32[1024]{0:T(1024)S(1)} %fusion.36), kind=kCustom, calls=%fused_computation.2.clone | custom fusion | bytes 528384 | tf_op jit(solution)/shard_map/jit(_take)/gather | solution.py:51
  23.2 0.2 select_convert_fusion
  23.4 0.2 copy.39
  23.6 3.2 %gather_fusion = bf16[1024,128]{1,0:T(8,128)(2,1)S(1)} fusion(bf16[4096,128]{1,0:T(8,128)(2,1)S(1)} %reshape.167, s32[1024]{0:T(1024)S(1)} %fusion.34), kind=kCustom, calls=%fused_computation.clone | custom fusion | bytes 528384 | tf_op jit(solution)/shard_map/jit(_take)/gather | solution.py:51
  26.8 0.2 select_convert_fusion.2
  27.0 0.2 copy.35
  27.2 3.2 %gather_fusion.1 = bf16[1024,128]{1,0:T(8,128)(2,1)S(1)} fusion(bf16[4096,128]{1,0:T(8,128)(2,1)S(1)} %reshape.167, s32[1024]{0:T(1024)S(1)} %fusion.35), kind=kCustom, calls=%fused_computation.1.clone | custom fusion | bytes 528384 | tf_op jit(solution)/shard_map/jit(_take)/gather | solution.py:51
  30.4 0.2 select_convert_fusion.1
  30.6 0.2 copy.37
  31.2 0.4 copy-done
  31.5 0.2 broadcast_in_dim.11
  32.0 14.7 %all_to_all.10 = bf16[8,144,2,64]{1,3,2,0:T(8,128)(2,1)S(1)} all-to-all(bf16[8,144,2,64]{1,3,2,0:T(8,128)(2,1)S(1)} %copy.40), channel_id=1, replica_groups=mesh['sub'=64,'grp'=8] {'grp'}, dimensions={0} | all-to-all | bytes 589824 | tf_op jit(solution)/shard_map/all_to_all | solution.py:64
  46.7 0.2 copy.57
  46.9 0.5 fusion.14
  47.4 0.2 copy.43
  47.6 39.1 %all_to_all.11 = bf16[64,8,2,128]{3,1,2,0:T(8,128)(2,1)S(1)} all-to-all(bf16[64,8,2,128]{3,1,2,0:T(8,128)(2,1)S(1)} %copy.44), channel_id=1, replica_groups=mesh['sub'=64,'grp'=8] {'sub'}, dimensions={0} | all-to-all | bytes 524288 | tf_op jit(solution)/shard_map/all_to_all | solution.py:76
  86.8 0.6 copy.46
  (26 shorter events, 0.9 us)
Async XLA Ops:
  30.9 0.7 copy-start
  30.9 0.7 copy-start.1

commit v4 on v3

--- a/solution.py
+++ b/solution.py
@@ -25,18 +25,27 @@
     return (right, left, window)
 
 
-def spectra_freq_major(frames, right, left, window):
+def rotation_tables(right):
     box = right.shape[1] // 2
-    count = frames.shape[0]
+    cos_t = jnp.transpose(right[:, :box])
+    sin_t = jnp.transpose(right[:, box:])
+    real_rows = jnp.stack([cos_t, -sin_t], axis=1)
+    imag_rows = jnp.stack([sin_t, cos_t], axis=1)
+    return jnp.stack([real_rows, imag_rows], axis=0)
+
+
+def spectra_tile_major(frames, right, window):
+    box = right.shape[1] // 2
+    count, patch = frames.shape[0], frames.shape[1]
     apodised = (frames.astype(jnp.float32) * window).astype(jnp.bfloat16)
     half = jnp.einsum("nij,jc->nic", apodised, right, preferred_element_type=jnp.float32).astype(
         jnp.bfloat16
     )
-    full = jnp.einsum("ki,nic->kcn", left, half, preferred_element_type=jnp.float32)
-    real_part = full[:box, :box] - full[box:, box:]
-    imag_part = full[:box, box:] + full[box:, :box]
-    spec = jnp.stack([real_part, imag_part], axis=2).astype(jnp.bfloat16)
-    return spec.reshape(box * box, 2 * count)
+    halves = half.reshape(count, patch, 2, box)
+    spec = jnp.einsum(
+        "pjqi,niqk->pjkn", rotation_tables(right), halves, preferred_element_type=jnp.float32
+    ).astype(jnp.bfloat16)
+    return jnp.transpose(spec, (0, 3, 1, 2)).reshape(2 * count, box * box)
 
 
 def local(tiles, dest_owner, dest_slot, triples):
@@ -47,8 +56,12 @@
     peers = lax.axis_size("sub")
     target = dest_owner[0] * OWN + dest_slot[0]
     right, left, window = make_tables(patch, BOX)
-    spec = spectra_freq_major(frames, right, left, window)
-    picked = [jnp.take(spec, triples[w], axis=0).astype(jnp.float32) for w in range(3)]
+    spec = spectra_tile_major(frames, right, window)
+    freq_ids = jnp.arange(spec.shape[1], dtype=jnp.int32)[:, None]
+    picked = []
+    for which in range(3):
+        select = (freq_ids == triples[which][None, :]).astype(jnp.bfloat16)
+        picked.append(jnp.transpose(jnp.dot(spec, select, preferred_element_type=jnp.float32)))
     ntri = triples.shape[1]
     first, second, third = [p.reshape(ntri, 2, count) for p in picked]
     prod_real = first[:, 0] * second[:, 0] - first[:, 1] * second[:, 1]

time: 87.7 us -> 75 us (0.86)
  local copies, waits for them, and re-layouts: 21.4 us -> 7.4 us
  matrix products: 5.42 us -> 12.1 us
  other arithmetic: 6.55 us -> 1.23 us
    gather x3 -> x0, local copies, waits for them, and re-layouts: 9.62 us -> none  [local(): jnp.take(spec, triples[w], axis=0).astype(jnp.float32)]
    dot_general x1 -> x5, matrix products: 4.95 us -> 11.6 us  [the longest x3 8.58 us: local(): jnp.dot(spec, select, preferred_element_type=jnp.float32)]
    convert_element_type x2 -> x1, local copies, waits for them, and re-layouts: 8.56 us -> 2.9 us  [spectra_tile_major(): spec = jnp.einsum('pjqi,niqk->pjkn', rotation_tables(right), halves, pref...]
    another operation x4, other arithmetic: 5.14 us -> 0.12 us  [the longest x1 0.1 us: local(): terms = jnp.stack([out_real, out_imag], axis=1).astype(jnp.bfloat16)]
    dot_general x0 -> x1, local copies, waits for them, and re-layouts: none -> 3.32 us  [local(): jnp.dot(spec, select, preferred_element_type=jnp.float32)]
where the time goes in v4:
time: 75 us; the launch traced here: 74.7 us
  blocking collectives  53.8 us (72%)
  matrix products  12.1 us (16%)
  local copies, waits for them, and re-layouts  7.4 us (10%)
  other arithmetic  1.23 us (2%)
    all_to_all x1, blocking collectives, local(): lax.all_to_all(shaped, 'sub', split_axis=0, concat_axis=0, tiled=True)  39.1 us
    all_to_all x1, blocking collectives, local(): lax.all_to_all(payload, 'grp', split_axis=0, concat_axis=0, tiled=True)  14.7 us
    dot_general x3, matrix products, local(): jnp.dot(spec, select, preferred_element_type=jnp.float32)  8.58 us
    dot_general x1, local copies, waits for them, and re-layouts, local(): jnp.dot(spec, select, preferred_element_type=jnp.float32)  3.32 us
    convert_element_type x1, local copies, waits for them, and re-layouts, spectra_tile_major(): spec = jnp.einsum('pjqi,niqk->pjkn', rotation_tables(right), halves, pref...  2.9 us
    dot_general x1, matrix products, spectra_tile_major(): jnp.einsum('nij,jc->nic', apodised, right, preferred_element_type=jnp.flo...  2.32 us

profile of v4, /device:TPU:6, one launch (start us, length us, event | category | flops | bytes accessed | tf_op | source)
XLA Modules:
  0.0 74.7 jit_solution(7327710127030548088)
XLA Ops:
  0.0 0.2 multiply_convert_fusion
  0.2 0.2 fusion.46
  0.4 0.2 multiply_convert_fusion.3
  0.7 0.1 broadcast_multiply_fusion
  0.8 2.3 %fusion.17 = bf16[64,128,128]{1,2,0:T(8,128)(2,1)S(1)} fusion(bf16[1,64,128,128]{3,2,1,0:T(8,128)(2,1)} %param.4, f32[128,128]{1,0:T(8,128)S(1)} %broadcast_multiply_fusion, bf16[128,64]{0,1:T(8,128)(2,1)S(1)} %get-tuple-element.16, bf16[128,64]{0,1:T(8,128)(2,1)S(1)} %get-tuple-element.15), kind=kOutput, calls=%fused_computation.18 | convolution fusion | flops 272695296 | bytes 4292608 | tf_op jit(solution)/shard_map/nij,jc->nic/dot_general | solution.py:41
  3.2 0.7 fusion.20
  3.9 2.9 %copy.11 = bf16[2,64,64,64]{3,2,1,0:T(8,128)(2,1)} copy(bf16[2,64,64,64]{2,3,0,1:T(8,128)(2,1)S(1)} %fusion.20) | data formatting | bytes 2097152 | tf_op jit(solution)/shard_map/convert_element_type | solution.py:47
  6.8 3.3 %dot_general.22 = bf16[2,64,4096]{2,1,0:T(8,128)(2,1)S(1)} reshape(bf16[2,64,64,64]{3,2,1,0:T(8,128)(2,1)} %copy.11) | data formatting | bytes 2097152 | tf_op jit(solution)/shard_map/dot_general | solution.py:64
  10.1 2.9 %fusion.3 = f32[1024,2,64]{0,2,1:T(8,128)S(1)} fusion(bf16[2,64,4096]{2,1,0:T(8,128)(2,1)S(1)} %dot_general.22, s32[1024]{0:T(1024)S(1)} %bitcast.83), kind=kOutput, calls=%fused_computation.6 | convolution fusion | flops 1077936128 | bytes 1576960 | tf_op jit(solution)/shard_map/dot_general | solution.py:64
  13.0 2.9 %fusion.5 = f32[1024,2,64]{0,2,1:T(8,128)S(1)} fusion(bf16[2,64,4096]{2,1,0:T(8,128)(2,1)S(1)} %dot_general.22, s32[1024]{0:T(1024)S(1)} %bitcast.82), kind=kOutput, calls=%fused_computation.7 | convolution fusion | flops 1077936128 | bytes 1576960 | tf_op jit(solution)/shard_map/dot_general | solution.py:64
  15.9 0.0 copy-start.1
  15.9 0.0 copy-start.2
  15.9 2.9 %fusion.7 = f32[1024,2,64]{0,2,1:T(8,128)S(1)} fusion(bf16[2,64,4096]{2,1,0:T(8,128)(2,1)S(1)} %dot_general.22, s32[1024]{0:T(1024)S(1)} %bitcast.81), kind=kOutput, calls=%fused_computation.8 | convolution fusion | flops 1077936128 | bytes 1576960 | tf_op jit(solution)/shard_map/dot_general | solution.py:64
  18.8 0.1 fusion.27
  19.0 0.1 copy_bitcast_fusion
  19.1 0.1 broadcast_in_dim.2
  19.2 0.1 pad_maximum_fusion
  19.3 14.7 %all_to_all.10 = bf16[8,144,2,64]{1,3,2,0:T(8,128)(2,1)S(1)} all-to-all(bf16[8,144,2,64]{1,3,2,0:T(8,128)(2,1)S(1)} %pad_maximum_fusion), channel_id=1, replica_groups=mesh['sub'=64,'grp'=8] {'grp'}, dimensions={0} | all-to-all | bytes 589824 | tf_op jit(solution)/shard_map/all_to_all | solution.py:77
  34.0 0.2 copy.25
  34.2 0.5 fusion.22
  34.7 0.2 copy.16
  34.9 39.1 %all_to_all.11 = bf16[64,8,2,128]{3,1,2,0:T(8,128)(2,1)S(1)} all-to-all(bf16[64,8,2,128]{3,1,2,0:T(8,128)(2,1)S(1)} %copy.17), channel_id=1, replica_groups=mesh['sub'=64,'grp'=8] {'sub'}, dimensions={0} | all-to-all | bytes 524288 | tf_op jit(solution)/shard_map/all_to_all | solution.py:89
  74.0 0.1 convert_reduce_fusion
  74.1 0.6 copy.19
  (15 shorter events, 0.2 us)
Async XLA Ops:
  6.8 3.3 %copy-start = (s32[3,1024]{1,0:T(4,128)S(1)}, s32[3,1024]{1,0:T(4,128)}, u32[]{:S(2)}) copy-start(s32[3,1024]{1,0:T(4,128)} %param.7) | copy-start | bytes 36868
  15.9 2.9 %copy-start.1 = (s32[1,64]{1,0:T(1,128)S(1)}, s32[1,64]{1,0:T(1,128)}, u32[]{:S(2)}) copy-start(s32[1,64]{1,0:T(1,128)} %param.5) | copy-start | bytes 772
  15.9 2.9 %copy-start.2 = (s32[1,64]{1,0:T(1,128)S(1)}, s32[1,64]{1,0:T(1,128)}, u32[]{:S(2)}) copy-start(s32[1,64]{1,0:T(1,128)} %param.6) | copy-start | bytes 772

commit v5 on v4

--- a/solution.py
+++ b/solution.py
@@ -57,10 +57,13 @@
     target = dest_owner[0] * OWN + dest_slot[0]
     right, left, window = make_tables(patch, BOX)
     spec = spectra_tile_major(frames, right, window)
-    freq_ids = jnp.arange(spec.shape[1], dtype=jnp.int32)[:, None]
+    freq_ids = jnp.arange(spec.shape[1], dtype=jnp.int16)[:, None]
+    one = jnp.ones((), jnp.bfloat16)
+    zero = jnp.zeros((), jnp.bfloat16)
     picked = []
     for which in range(3):
-        select = (freq_ids == triples[which][None, :]).astype(jnp.bfloat16)
+        hit = freq_ids == triples[which].astype(jnp.int16)[None, :]
+        select = jnp.where(hit, one, zero)
         picked.append(jnp.transpose(jnp.dot(spec, select, preferred_element_type=jnp.float32)))
     ntri = triples.shape[1]
     first, second, third = [p.reshape(ntri, 2, count) for p in picked]

time: 75 us -> 70.2 us (0.936)
  matrix products: 12.1 us -> 7.29 us
    dot_general x3, matrix products: 8.58 us -> 3.77 us  [local(): jnp.dot(spec, select, preferred_element_type=jnp.float32)]
where the time goes in v5:
time: 70.2 us; the launch traced here: 69.9 us
  blocking collectives  53.8 us (77%)
  local copies, waits for them, and re-layouts  7.43 us (11%)
  matrix products  7.29 us (10%)
  other arithmetic  1.22 us (2%)
    all_to_all x1, blocking collectives, local(): lax.all_to_all(shaped, 'sub', split_axis=0, concat_axis=0, tiled=True)  39.1 us
    all_to_all x1, blocking collectives, local(): lax.all_to_all(payload, 'grp', split_axis=0, concat_axis=0, tiled=True)  14.7 us
    dot_general x3, matrix products, local(): jnp.dot(spec, select, preferred_element_type=jnp.float32)  3.77 us
    dot_general x1, local copies, waits for them, and re-layouts, local(): jnp.dot(spec, select, preferred_element_type=jnp.float32)  3.32 us
    convert_element_type x1, local copies, waits for them, and re-layouts, spectra_tile_major(): spec = jnp.einsum('pjqi,niqk->pjkn', rotation_tables(right), halves, pref...  2.89 us
    dot_general x1, matrix products, spectra_tile_major(): jnp.einsum('nij,jc->nic', apodised, right, preferred_element_type=jnp.flo...  2.32 us

profile of v5, /device:TPU:6, one launch (start us, length us, event | category | flops | bytes accessed | tf_op | source)
XLA Modules:
  0.0 69.9 jit_solution(12955041098452469837)
XLA Ops:
  0.0 0.2 multiply_convert_fusion
  0.2 0.2 fusion.52
  0.4 0.2 multiply_convert_fusion.3
  0.7 0.1 broadcast_multiply_fusion
  0.8 2.3 %fusion.23 = bf16[64,128,128]{1,2,0:T(8,128)(2,1)S(1)} fusion(bf16[1,64,128,128]{3,2,1,0:T(8,128)(2,1)} %param.4, f32[128,128]{1,0:T(8,128)S(1)} %broadcast_multiply_fusion, bf16[128,64]{0,1:T(8,128)(2,1)S(1)} %get-tuple-element.16, bf16[128,64]{0,1:T(8,128)(2,1)S(1)} %get-tuple-element.15), kind=kOutput, calls=%fused_computation.24 | convolution fusion | flops 272695296 | bytes 4292608 | tf_op jit(solution)/shard_map/nij,jc->nic/dot_general | solution.py:41
  3.2 0.7 %fusion.26 = bf16[2,64,64,64]{2,3,0,1:T(8,128)(2,1)S(1)} fusion(bf16[64,128,2,64,1]{1,3,2,4,0:T(8,128)(2,1)S(1)} %bitcast.76, bf16[1,64,2,128]{3,1,2,0:T(8,128)(2,1)S(1)} %get-tuple-element.12, bf16[1,64,2,128]{3,1,2,0:T(8,128)(2,1)S(1)} %get-tuple-element.11), kind=kOutput, calls=%fused_computation.25 | convolution fusion | flops 269090816 | bytes 3211264 | tf_op jit(solution)/shard_map/pjqi,niqk->pjkn/dot_general | solution.py:45
  3.9 2.9 %copy.11 = bf16[2,64,64,64]{3,2,1,0:T(8,128)(2,1)} copy(bf16[2,64,64,64]{2,3,0,1:T(8,128)(2,1)S(1)} %fusion.26) | data formatting | bytes 2097152 | tf_op jit(solution)/shard_map/convert_element_type | solution.py:47
  6.8 3.3 %dot_general.22 = bf16[2,64,4096]{2,1,0:T(8,128)(2,1)S(1)} reshape(bf16[2,64,64,64]{3,2,1,0:T(8,128)(2,1)} %copy.11) | data formatting | bytes 2097152 | tf_op jit(solution)/shard_map/dot_general | solution.py:67
  10.2 1.3 %fusion.3 = f32[1024,2,64]{0,2,1:T(8,128)S(1)} fusion(bf16[2,64,4096]{2,1,0:T(8,128)(2,1)S(1)} %dot_general.22, s16[1024]{0:T(1024)(128)(2,1)S(1)} %get-tuple-element.5), kind=kOutput, calls=%fused_computation.6 | convolution fusion | flops 1082130432 | bytes 1574912 | tf_op jit(solution)/shard_map/dot_general | solution.py:67
  11.4 1.3 %fusion.5 = f32[1024,2,64]{0,2,1:T(8,128)S(1)} fusion(bf16[2,64,4096]{2,1,0:T(8,128)(2,1)S(1)} %dot_general.22, s16[1024]{0:T(1024)(128)(2,1)S(1)} %get-tuple-element.6), kind=kOutput, calls=%fused_computation.7 | convolution fusion | flops 1082130432 | bytes 1574912 | tf_op jit(solution)/shard_map/dot_general | solution.py:67
  12.7 0.0 copy-start.1
  12.7 0.0 copy-start.2
  12.7 1.3 %fusion.7 = f32[1024,2,64]{0,2,1:T(8,128)S(1)} fusion(bf16[2,64,4096]{2,1,0:T(8,128)(2,1)S(1)} %dot_general.22, s16[1024]{0:T(1024)(128)(2,1)S(1)} %get-tuple-element.7), kind=kOutput, calls=%fused_computation.8 | convolution fusion | flops 1082130432 | bytes 1574912 | tf_op jit(solution)/shard_map/dot_general | solution.py:67
  14.1 0.1 fusion.33
  14.2 0.1 copy_bitcast_fusion
  14.3 0.1 broadcast_in_dim.16
  14.4 0.1 pad_maximum_fusion
  14.5 14.7 %all_to_all.10 = bf16[8,144,2,64]{1,3,2,0:T(8,128)(2,1)S(1)} all-to-all(bf16[8,144,2,64]{1,3,2,0:T(8,128)(2,1)S(1)} %pad_maximum_fusion), channel_id=1, replica_groups=mesh['sub'=64,'grp'=8] {'grp'}, dimensions={0} | all-to-all | bytes 589824 | tf_op jit(solution)/shard_map/all_to_all | solution.py:80
  29.2 0.2 copy.25
  29.4 0.5 fusion.28
  29.9 0.2 copy.16
  30.1 39.1 %all_to_all.11 = bf16[64,8,2,128]{3,1,2,0:T(8,128)(2,1)S(1)} all-to-all(bf16[64,8,2,128]{3,1,2,0:T(8,128)(2,1)S(1)} %copy.17), channel_id=1, replica_groups=mesh['sub'=64,'grp'=8] {'sub'}, dimensions={0} | all-to-all | bytes 524288 | tf_op jit(solution)/shard_map/all_to_all | solution.py:92
  69.2 0.1 convert_reduce_fusion
  69.3 0.6 copy.19
  (16 shorter events, 0.2 us)
Async XLA Ops:
  6.8 3.3 %copy-start = (s32[3,1024]{1,0:T(4,128)S(1)}, s32[3,1024]{1,0:T(4,128)}, u32[]{:S(2)}) copy-start(s32[3,1024]{1,0:T(4,128)} %param.7) | copy-start | bytes 36868
  12.7 1.3 %copy-start.1 = (s32[1,64]{1,0:T(1,128)S(1)}, s32[1,64]{1,0:T(1,128)}, u32[]{:S(2)}) copy-start(s32[1,64]{1,0:T(1,128)} %param.5) | copy-start | bytes 772
  12.7 1.3 %copy-start.2 = (s32[1,64]{1,0:T(1,128)S(1)}, s32[1,64]{1,0:T(1,128)}, u32[]{:S(2)}) copy-start(s32[1,64]{1,0:T(1,128)} %param.6) | copy-start | bytes 772

commit v6 on v5

--- a/solution.py
+++ b/solution.py
@@ -3,6 +3,8 @@
 import jax
 import jax.numpy as jnp
 from jax import lax
+from jax.experimental import pallas as pl
+from jax.experimental.pallas import tpu as pltpu
 from jax.sharding import PartitionSpec as P
 
 BOX = 64
@@ -43,9 +45,30 @@
     )
     halves = half.reshape(count, patch, 2, box)
     spec = jnp.einsum(
-        "pjqi,niqk->pjkn", rotation_tables(right), halves, preferred_element_type=jnp.float32
+        "pjqi,niqk->jpnk", rotation_tables(right), halves, preferred_element_type=jnp.float32
     ).astype(jnp.bfloat16)
-    return jnp.transpose(spec, (0, 3, 1, 2)).reshape(2 * count, box * box)
+    return flatten_rows(spec)
+
+
+def flatten_kernel(x_ref, o_ref):
+    rows = x_ref.shape[1] * x_ref.shape[2]
+    width = x_ref.shape[3]
+    for pair in range(x_ref.shape[0] // 2):
+        lo = x_ref[2 * pair].reshape(rows, width)
+        hi = x_ref[2 * pair + 1].reshape(rows, width)
+        o_ref[:, pair * 2 * width : (pair + 1) * 2 * width] = jnp.concatenate([lo, hi], axis=1)
+
+
+def flatten_rows(spec):
+    j1, parts, count, j2 = spec.shape
+    size = spec.size * spec.dtype.itemsize
+    return pl.pallas_call(
+        flatten_kernel,
+        out_shape=jax.ShapeDtypeStruct((parts * count, j1 * j2), spec.dtype),
+        in_specs=[pl.BlockSpec(memory_space=pltpu.VMEM)],
+        out_specs=pl.BlockSpec(memory_space=pltpu.VMEM),
+        cost_estimate=pl.CostEstimate(flops=0, transcendentals=0, bytes_accessed=2 * size),
+    )(spec)
 
 
 def local(tiles, dest_owner, dest_slot, triples):

time: 70.2 us -> 72.1 us (1.027)
  Pallas kernels: 0 us -> 2.96 us
  local copies, waits for them, and re-layouts: 7.43 us -> 5.15 us
  matrix products: 7.29 us -> 8.59 us
    pallas_call x0 -> x1, Pallas kernels: none -> 2.96 us  [flatten_rows(): pl.pallas_call(flatten_kernel, out_shape=jax.ShapeDtypeStruct((parts * co...]
    convert_element_type x1 -> x0, local copies, waits for them, and re-layouts: 2.89 us -> none  [spectra_tile_major(): spec = jnp.einsum('pjqi,niqk->pjkn', rotation_tables(right), halves, pref...]
    dot_general x3, matrix products: 3.77 us -> 5.08 us  [local(): jnp.dot(spec, select, preferred_element_type=jnp.float32)]
where the time goes in v6:
time: 72.1 us; the launch traced here: 71.9 us
  blocking collectives  53.8 us (75%)
  matrix products  8.59 us (12%)
  local copies, waits for them, and re-layouts  5.15 us (7%)
  Pallas kernels  2.96 us (4%)
  other arithmetic  1.2 us (2%)
    all_to_all x1, blocking collectives, local(): lax.all_to_all(shaped, 'sub', split_axis=0, concat_axis=0, tiled=True)  39.1 us
    all_to_all x1, blocking collectives, local(): lax.all_to_all(payload, 'grp', split_axis=0, concat_axis=0, tiled=True)  14.7 us
    dot_general x3, matrix products, local(): jnp.dot(spec, select, preferred_element_type=jnp.float32)  5.08 us
    dot_general x1, local copies, waits for them, and re-layouts, spectra_tile_major(): jnp.einsum('pjqi,niqk->jpnk', rotation_tables(right), halves, preferred_e...  3.31 us
    pallas_call x1, Pallas kernels, flatten_rows(): pl.pallas_call(flatten_kernel, out_shape=jax.ShapeDtypeStruct((parts * co...  2.96 us
    dot_general x1, matrix products, spectra_tile_major(): jnp.einsum('nij,jc->nic', apodised, right, preferred_element_type=jnp.flo...  2.32 us

profile of v6, /device:TPU:6, one launch (start us, length us, event | category | flops | bytes accessed | tf_op | source)
XLA Modules:
  0.0 71.9 jit_solution(12558918181619306500)
XLA Ops:
  0.0 0.2 multiply_convert_fusion
  0.2 0.2 fusion.48
  0.4 0.2 multiply_convert_fusion.3
  0.7 0.1 broadcast_multiply_fusion
  0.8 2.3 %fusion.20 = bf16[64,128,128]{1,2,0:T(8,128)(2,1)S(1)} fusion(bf16[1,64,128,128]{3,2,1,0:T(8,128)(2,1)} %param.4, f32[128,128]{1,0:T(8,128)S(1)} %broadcast_multiply_fusion, bf16[128,64]{0,1:T(8,128)(2,1)S(1)} %get-tuple-element.16, bf16[128,64]{0,1:T(8,128)(2,1)S(1)} %get-tuple-element.15), kind=kOutput, calls=%fused_computation.25 | convolution fusion | flops 272695296 | bytes 4292608 | tf_op jit(solution)/shard_map/nij,jc->nic/dot_general | solution.py:43
  3.2 0.7 %convolution_bitcast_fusion = bf16[64,64,2,64]{3,1,2,0:T(8,128)(2,1)S(1)} fusion(bf16[64,128,2,64,1]{1,3,2,4,0:T(8,128)(2,1)S(1)} %bitcast.72, bf16[1,64,2,128]{3,1,2,0:T(8,128)(2,1)S(1)} %get-tuple-element.12, bf16[1,64,2,128]{3,1,2,0:T(8,128)(2,1)S(1)} %get-tuple-element.11), kind=kOutput, calls=%fused_computation.20 | convolution fusion | flops 268566528 | bytes 3211264 | tf_op jit(solution)/shard_map/pjqi,niqk->jpnk/dot_general | solution.py:47
  3.9 3.3 %copy.10 = bf16[64,64,2,64]{1,0,2,3:T(8,128)(2,1)} copy(bf16[64,64,2,64]{3,1,2,0:T(8,128)(2,1)S(1)} %convolution_bitcast_fusion) | data formatting | bytes 2097152 | tf_op jit(solution)/shard_map/pjqi,niqk->jpnk/dot_general | solution.py:47
  7.2 3.0 %shard_map.46 = bf16[128,4096]{1,0:T(8,128)(2,1)} custom-call(bf16[64,2,64,64]{3,2,1,0:T(8,128)(2,1)} %bitcast.73), custom_call_target="tpu_custom_call" | custom-call | bytes 2097152 | tf_op jit(solution)/shard_map/pallas_call | solution.py:65
  10.2 2.6 %fusion.2 = f32[1024,128]{0,1:T(8,128)S(1)} fusion(bf16[128,4096]{1,0:T(8,128)(2,1)} %shard_map.46, s16[1024]{0:T(1024)(128)(2,1)S(1)} %get-tuple-element.5), kind=kOutput, calls=%fused_computation.5 | convolution fusion | flops 1082130432 | bytes 1574912 | tf_op jit(solution)/shard_map/dot_general | solution.py:90
  12.8 1.3 %fusion = f32[1024,128]{0,1:T(8,128)S(1)} fusion(bf16[128,4096]{1,0:T(8,128)(2,1)S(1)} %copy-done, s16[1024]{0:T(1024)(128)(2,1)S(1)} %get-tuple-element.7), kind=kOutput, calls=%fused_computation.3 | convolution fusion | flops 1082130432 | bytes 1574912 | tf_op jit(solution)/shard_map/dot_general | solution.py:90
  14.1 1.3 %fusion.1 = f32[1024,128]{0,1:T(8,128)S(1)} fusion(bf16[128,4096]{1,0:T(8,128)(2,1)S(1)} %copy-done, s16[1024]{0:T(1024)(128)(2,1)S(1)} %get-tuple-element.6), kind=kOutput, calls=%fused_computation.4 | convolution fusion | flops 1082130432 | bytes 1574912 | tf_op jit(solution)/shard_map/dot_general | solution.py:90
  15.4 0.1 fusion.29
  15.5 0.1 fusion.30
  15.6 0.4 copy-done.2
  16.0 0.2 broadcast_in_dim.16
  16.2 0.1 pad_maximum_fusion
  16.4 0.1 copy.11
  16.5 14.7 %all_to_all.10 = bf16[8,144,2,64]{1,3,2,0:T(8,128)(2,1)S(1)} all-to-all(bf16[8,144,2,64]{1,3,2,0:T(8,128)(2,1)S(1)} %copy.11), channel_id=1, replica_groups=mesh['sub'=64,'grp'=8] {'grp'}, dimensions={0} | all-to-all | bytes 589824 | tf_op jit(solution)/shard_map/all_to_all | solution.py:103
  31.2 0.2 copy.23
  31.4 0.5 fusion.24
  31.8 0.2 copy.14
  32.1 39.1 %all_to_all.11 = bf16[64,8,2,128]{3,1,2,0:T(8,128)(2,1)S(1)} all-to-all(bf16[64,8,2,128]{3,1,2,0:T(8,128)(2,1)S(1)} %copy.15), channel_id=1, replica_groups=mesh['sub'=64,'grp'=8] {'sub'}, dimensions={0} | all-to-all | bytes 524288 | tf_op jit(solution)/shard_map/all_to_all | solution.py:115
  71.2 0.1 convert_reduce_fusion
  71.3 0.6 copy.17
  (21 shorter events, 0.3 us)
Async XLA Ops:
  7.2 3.0 %copy-start.1 = (s32[3,1024]{1,0:T(4,128)S(1)}, s32[3,1024]{1,0:T(4,128)}, u32[]{:S(2)}) copy-start(s32[3,1024]{1,0:T(4,128)} %param.7) | copy-start | bytes 36868
  10.2 2.6 %copy-start = (bf16[128,4096]{1,0:T(8,128)(2,1)S(1)}, bf16[128,4096]{1,0:T(8,128)(2,1)}, u32[]{:S(2)}) copy-start(bf16[128,4096]{1,0:T(8,128)(2,1)} %shard_map.46) | copy-start | bytes 3145732
  15.3 0.7 copy-start.2
  15.4 0.7 copy-start.3

commit v7 on v5

--- a/solution.py
+++ b/solution.py
@@ -43,9 +43,9 @@
     )
     halves = half.reshape(count, patch, 2, box)
     spec = jnp.einsum(
-        "pjqi,niqk->pjkn", rotation_tables(right), halves, preferred_element_type=jnp.float32
+        "pjqi,niqk->npkj", rotation_tables(right), halves, preferred_element_type=jnp.float32
     ).astype(jnp.bfloat16)
-    return jnp.transpose(spec, (0, 3, 1, 2)).reshape(2 * count, box * box)
+    return spec.reshape(count * 2, box * box)
 
 
 def local(tiles, dest_owner, dest_slot, triples):
@@ -61,16 +61,17 @@
     one = jnp.ones((), jnp.bfloat16)
     zero = jnp.zeros((), jnp.bfloat16)
     picked = []
+    swapped = (triples % BOX) * BOX + triples // BOX
     for which in range(3):
-        hit = freq_ids == triples[which].astype(jnp.int16)[None, :]
+        hit = freq_ids == swapped[which].astype(jnp.int16)[None, :]
         select = jnp.where(hit, one, zero)
         picked.append(jnp.transpose(jnp.dot(spec, select, preferred_element_type=jnp.float32)))
     ntri = triples.shape[1]
-    first, second, third = [p.reshape(ntri, 2, count) for p in picked]
-    prod_real = first[:, 0] * second[:, 0] - first[:, 1] * second[:, 1]
-    prod_imag = first[:, 0] * second[:, 1] + first[:, 1] * second[:, 0]
-    out_real = prod_real * third[:, 0] + prod_imag * third[:, 1]
-    out_imag = prod_imag * third[:, 0] - prod_real * third[:, 1]
+    first, second, third = [p.reshape(ntri, count, 2) for p in picked]
+    prod_real = first[..., 0] * second[..., 0] - first[..., 1] * second[..., 1]
+    prod_imag = first[..., 0] * second[..., 1] + first[..., 1] * second[..., 0]
+    out_real = prod_real * third[..., 0] + prod_imag * third[..., 1]
+    out_imag = prod_imag * third[..., 0] - prod_real * third[..., 1]
     terms = jnp.stack([out_real, out_imag], axis=1).astype(jnp.bfloat16)
     block = ntri // groups
     terms = terms.reshape(groups, block, 2, count)

time: 70.2 us -> 66.1 us (0.942)
  local copies, waits for them, and re-layouts: 7.43 us -> 3.12 us
    convert_element_type x1 -> x0, local copies, waits for them, and re-layouts: 2.89 us -> none  [spectra_tile_major(): spec = jnp.einsum('pjqi,niqk->pjkn', rotation_tables(right), halves, pref...]
    dot_general x1, local copies, waits for them, and re-layouts: 3.32 us -> 1.5 us  [local(): jnp.dot(spec, select, preferred_element_type=jnp.float32)]
where the time goes in v7:
time: 66.1 us; the launch traced here: 65.9 us
  blocking collectives  53.8 us (81%)
  matrix products  7.58 us (11%)
  local copies, waits for them, and re-layouts  3.12 us (5%)
  other arithmetic  1.24 us (2%)
    all_to_all x1, blocking collectives, local(): lax.all_to_all(shaped, 'sub', split_axis=0, concat_axis=0, tiled=True)  39.1 us
    all_to_all x1, blocking collectives, local(): lax.all_to_all(payload, 'grp', split_axis=0, concat_axis=0, tiled=True)  14.7 us
    dot_general x3, matrix products, local(): jnp.dot(spec, select, preferred_element_type=jnp.float32)  4.07 us
    dot_general x1, matrix products, spectra_tile_major(): jnp.einsum('nij,jc->nic', apodised, right, preferred_element_type=jnp.flo...  2.32 us
    dot_general x1, local copies, waits for them, and re-layouts, local(): jnp.dot(spec, select, preferred_element_type=jnp.float32)  1.5 us

profile of v7, /device:TPU:6, one launch (start us, length us, event | category | flops | bytes accessed | tf_op | source)
XLA Modules:
  0.0 65.9 jit_solution(10075208478524449376)
XLA Ops:
  0.0 0.2 multiply_convert_fusion
  0.2 0.2 fusion.60
  0.4 0.2 multiply_convert_fusion.3
  0.7 0.1 broadcast_multiply_fusion
  0.8 2.3 %fusion.23 = bf16[64,128,128]{1,2,0:T(8,128)(2,1)S(1)} fusion(bf16[1,64,128,128]{3,2,1,0:T(8,128)(2,1)} %param.4, f32[128,128]{1,0:T(8,128)S(1)} %broadcast_multiply_fusion, bf16[128,64]{0,1:T(8,128)(2,1)S(1)} %get-tuple-element.16, bf16[128,64]{0,1:T(8,128)(2,1)S(1)} %get-tuple-element.15), kind=kOutput, calls=%fused_computation.24 | convolution fusion | flops 272695296 | bytes 4292608 | tf_op jit(solution)/shard_map/nij,jc->nic/dot_general | solution.py:41
  3.2 0.7 %fusion.26 = bf16[64,2,64,64]{3,2,1,0:T(8,128)(2,1)S(1)} fusion(bf16[64,128,2,64,1]{1,3,2,4,0:T(8,128)(2,1)S(1)} %bitcast.78, bf16[1,64,2,128]{3,1,2,0:T(8,128)(2,1)S(1)} %get-tuple-element.12, bf16[1,64,2,128]{3,1,2,0:T(8,128)(2,1)S(1)} %get-tuple-element.11), kind=kOutput, calls=%fused_computation.25 | convolution fusion | flops 269090816 | bytes 3211264 | tf_op jit(solution)/shard_map/pjqi,niqk->npkj/dot_general | solution.py:45
  3.9 1.5 %dot_general.22 = bf16[64,2,4096]{2,1,0:T(2,128)(2,1)S(1)} reshape(bf16[64,2,64,64]{3,2,1,0:T(8,128)(2,1)S(1)} %fusion.26) | data formatting | bytes 2097152 | tf_op jit(solution)/shard_map/dot_general | solution.py:68
  5.5 1.4 %fusion.3 = f32[1024,64,2]{0,1,2:T(8,128)S(1)} fusion(s16[1024]{0:T(1024)(128)(2,1)S(1)} %get-tuple-element.5, bf16[64,2,4096]{2,1,0:T(2,128)(2,1)S(1)} %dot_general.22), kind=kOutput, calls=%fused_computation.6 | convolution fusion | flops 1082130432 | bytes 1574912 | tf_op jit(solution)/shard_map/dot_general | solution.py:68
  6.9 1.4 %fusion.5 = f32[1024,64,2]{0,1,2:T(8,128)S(1)} fusion(s16[1024]{0:T(1024)(128)(2,1)S(1)} %get-tuple-element.6, bf16[64,2,4096]{2,1,0:T(2,128)(2,1)S(1)} %dot_general.22), kind=kOutput, calls=%fused_computation.7 | convolution fusion | flops 1082130432 | bytes 1574912 | tf_op jit(solution)/shard_map/dot_general | solution.py:68
  8.2 1.4 %fusion.7 = f32[1024,64,2]{0,1,2:T(8,128)S(1)} fusion(s16[1024]{0:T(1024)(128)(2,1)S(1)} %get-tuple-element.7, bf16[64,2,4096]{2,1,0:T(2,128)(2,1)S(1)} %dot_general.22), kind=kOutput, calls=%fused_computation.8 | convolution fusion | flops 1082130432 | bytes 1574912 | tf_op jit(solution)/shard_map/dot_general | solution.py:68
  9.6 0.0 copy-start.1
  9.6 0.1 fusion.36
  9.8 0.1 fusion.37
  10.0 0.3 copy-done.1
  10.3 0.0 copy-done.2
  10.3 0.1 broadcast_in_dim.16
  10.4 0.1 pad_maximum_fusion
  10.5 14.7 %all_to_all.10 = bf16[8,144,2,64]{1,3,2,0:T(8,128)(2,1)S(1)} all-to-all(bf16[8,144,2,64]{1,3,2,0:T(8,128)(2,1)S(1)} %pad_maximum_fusion), channel_id=1, replica_groups=mesh['sub'=64,'grp'=8] {'grp'}, dimensions={0} | all-to-all | bytes 589824 | tf_op jit(solution)/shard_map/all_to_all | solution.py:81
  25.3 0.2 copy.32
  25.4 0.5 fusion.28
  25.9 0.2 copy.23
  26.2 39.1 %all_to_all.11 = bf16[64,8,2,128]{3,1,2,0:T(8,128)(2,1)S(1)} all-to-all(bf16[64,8,2,128]{3,1,2,0:T(8,128)(2,1)S(1)} %copy.24), channel_id=1, replica_groups=mesh['sub'=64,'grp'=8] {'sub'}, dimensions={0} | all-to-all | bytes 524288 | tf_op jit(solution)/shard_map/all_to_all | solution.py:93
  65.3 0.1 convert_reduce_fusion
  65.3 0.6 copy.26
  (19 shorter events, 0.4 us)
Async XLA Ops:
  3.9 1.5 %copy-start = (s32[3,1024]{1,0:T(4,128)S(1)}, s32[3,1024]{1,0:T(4,128)}, u32[]{:S(2)}) copy-start(s32[3,1024]{1,0:T(4,128)} %param.7) | copy-start | bytes 36868
  9.6 0.7 copy-start.1
  9.6 0.7 %copy-start.2 = (s32[1,64]{1,0:T(1,128)S(1)}, s32[1,64]{1,0:T(1,128)}, u32[]{:S(2)}) copy-start(s32[1,64]{1,0:T(1,128)} %param.6) | copy-start | bytes 772

commit v8 on v5

--- a/solution.py
+++ b/solution.py
@@ -43,9 +43,9 @@
     )
     halves = half.reshape(count, patch, 2, box)
     spec = jnp.einsum(
-        "pjqi,niqk->pjkn", rotation_tables(right), halves, preferred_element_type=jnp.float32
+        "pjqi,niqk->npkj", rotation_tables(right), halves, preferred_element_type=jnp.float32
     ).astype(jnp.bfloat16)
-    return jnp.transpose(spec, (0, 3, 1, 2)).reshape(2 * count, box * box)
+    return spec.reshape(count * 2, box * box)
 
 
 def local(tiles, dest_owner, dest_slot, triples):
@@ -54,39 +54,39 @@
     patch = frames.shape[-1]
     groups = lax.axis_size("grp")
     peers = lax.axis_size("sub")
-    target = dest_owner[0] * OWN + dest_slot[0]
     right, left, window = make_tables(patch, BOX)
     spec = spectra_tile_major(frames, right, window)
     freq_ids = jnp.arange(spec.shape[1], dtype=jnp.int16)[:, None]
     one = jnp.ones((), jnp.bfloat16)
     zero = jnp.zeros((), jnp.bfloat16)
     picked = []
+    swapped = (triples % BOX) * BOX + triples // BOX
     for which in range(3):
-        hit = freq_ids == triples[which].astype(jnp.int16)[None, :]
+        hit = freq_ids == swapped[which].astype(jnp.int16)[None, :]
         select = jnp.where(hit, one, zero)
-        picked.append(jnp.transpose(jnp.dot(spec, select, preferred_element_type=jnp.float32)))
+        picked.append(jnp.dot(spec, select, preferred_element_type=jnp.float32))
     ntri = triples.shape[1]
-    first, second, third = [p.reshape(ntri, 2, count) for p in picked]
+    first, second, third = [p.reshape(count, 2, ntri) for p in picked]
     prod_real = first[:, 0] * second[:, 0] - first[:, 1] * second[:, 1]
     prod_imag = first[:, 0] * second[:, 1] + first[:, 1] * second[:, 0]
     out_real = prod_real * third[:, 0] + prod_imag * third[:, 1]
     out_imag = prod_imag * third[:, 0] - prod_real * third[:, 1]
-    terms = jnp.stack([out_real, out_imag], axis=1).astype(jnp.bfloat16)
+    terms = jnp.stack([out_real, out_imag], axis=0).astype(jnp.bfloat16)
     block = ntri // groups
-    terms = terms.reshape(groups, block, 2, count)
-    label = jnp.stack([dest_owner[0], dest_slot[0]]).astype(jnp.bfloat16)
-    marks = jnp.broadcast_to(label[None, None, :, :], (groups, 16, 2, count))
-    payload = jnp.concatenate([terms, marks], axis=1)
+    terms = jnp.transpose(terms.reshape(2, count, groups, block), (2, 0, 1, 3))
+    label = jnp.concatenate([dest_owner[0], dest_slot[0]]).astype(jnp.bfloat16)
+    marks = jnp.broadcast_to(label[None, None, None, :], (groups, 2, 8, 2 * count))
+    payload = jnp.concatenate([terms, marks], axis=2)
     got = lax.all_to_all(payload, "grp", split_axis=0, concat_axis=0, tiled=True)
-    got_terms = got[:, :block]
-    got_label = got[:, block].astype(jnp.int32)
-    got_marks = got_label[:, 0, :] * OWN + got_label[:, 1, :]
+    got_terms = got[:, :, :count]
+    got_label = got[:, 0, count].astype(jnp.int32)
+    got_marks = got_label[:, :count] * OWN + got_label[:, count:]
     rows = peers * OWN
     onehot = (
         got_marks[None, :, :] == jnp.arange(rows, dtype=jnp.int32)[:, None, None]
     ).astype(jnp.bfloat16)
     partial_value = jnp.einsum(
-        "rgn,gtcn->rct", onehot, got_terms, preferred_element_type=jnp.float32
+        "rgn,gcnt->rct", onehot, got_terms, preferred_element_type=jnp.float32
     )
     shaped = partial_value.astype(jnp.bfloat16).reshape(peers, OWN, 2, block)
     gathered = lax.all_to_all(shaped, "sub", split_axis=0, concat_axis=0, tiled=True)

time: 70.2 us -> 64.5 us (0.919)
  local copies, waits for them, and re-layouts: 7.43 us -> 2.6 us
  blocking collectives: 53.8 us -> 51.6 us
  matrix products: 7.29 us -> 8.5 us
    convert_element_type x2 -> x0, local copies, waits for them, and re-layouts: 3.06 us -> none  [the longest x1 2.89 us: spectra_tile_major(): spec = jnp.einsum('pjqi,niqk->pjkn', rotation_tables(right), halves, pref...]
    all_to_all x1, blocking collectives: 14.7 us -> 12.2 us  [local(): lax.all_to_all(payload, 'grp', split_axis=0, concat_axis=0, tiled=True)]
    dot_general x1, local copies, waits for them, and re-layouts: 3.32 us -> 1.5 us  [local(): picked.append(jnp.dot(spec, select, preferred_element_type=jnp.float32))]
    dot_general x5, matrix products: 4.97 us -> 6.18 us  [the longest x3 4.91 us: local(): picked.append(jnp.dot(spec, select, preferred_element_type=jnp.float32))]
where the time goes in v8:
time: 64.5 us; the launch traced here: 64.3 us
  blocking collectives  51.6 us (80%)
  matrix products  8.5 us (13%)
  local copies, waits for them, and re-layouts  2.6 us (4%)
  other arithmetic  1.31 us (2%)
    all_to_all x1, blocking collectives, local(): lax.all_to_all(shaped, 'sub', split_axis=0, concat_axis=0, tiled=True)  39.5 us
    all_to_all x1, blocking collectives, local(): lax.all_to_all(payload, 'grp', split_axis=0, concat_axis=0, tiled=True)  12.2 us
    dot_general x3, matrix products, local(): picked.append(jnp.dot(spec, select, preferred_element_type=jnp.float32))  4.91 us
    dot_general x1, matrix products, spectra_tile_major(): jnp.einsum('nij,jc->nic', apodised, right, preferred_element_type=jnp.flo...  2.32 us
    dot_general x1, local copies, waits for them, and re-layouts, local(): picked.append(jnp.dot(spec, select, preferred_element_type=jnp.float32))  1.5 us

profile of v8, /device:TPU:6, one launch (start us, length us, event | category | flops | bytes accessed | tf_op | source)
XLA Modules:
  0.0 64.3 jit_solution(5615174560433250478)
XLA Ops:
  0.0 0.2 multiply_convert_fusion
  0.2 0.2 fusion.59
  0.4 0.2 multiply_convert_fusion.3
  0.7 0.1 broadcast_multiply_fusion
  0.8 2.3 %fusion.23 = bf16[64,128,128]{1,2,0:T(8,128)(2,1)S(1)} fusion(bf16[1,64,128,128]{3,2,1,0:T(8,128)(2,1)} %param.4, f32[128,128]{1,0:T(8,128)S(1)} %broadcast_multiply_fusion, bf16[128,64]{0,1:T(8,128)(2,1)S(1)} %get-tuple-element.16, bf16[128,64]{0,1:T(8,128)(2,1)S(1)} %get-tuple-element.15), kind=kOutput, calls=%fused_computation.24 | convolution fusion | flops 272695296 | bytes 4292608 | tf_op jit(solution)/shard_map/nij,jc->nic/dot_general | solution.py:41
  3.2 0.7 %fusion.26 = bf16[64,2,64,64]{3,2,1,0:T(8,128)(2,1)S(1)} fusion(bf16[64,128,2,64,1]{1,3,2,4,0:T(8,128)(2,1)S(1)} %bitcast.77, bf16[1,64,2,128]{3,1,2,0:T(8,128)(2,1)S(1)} %get-tuple-element.12, bf16[1,64,2,128]{3,1,2,0:T(8,128)(2,1)S(1)} %get-tuple-element.11), kind=kOutput, calls=%fused_computation.25 | convolution fusion | flops 269090816 | bytes 3211264 | tf_op jit(solution)/shard_map/pjqi,niqk->npkj/dot_general | solution.py:45
  3.9 0.0 copy-start
  3.9 1.5 %dot_general.22 = bf16[64,2,4096]{2,1,0:T(2,128)(2,1)S(1)} reshape(bf16[64,2,64,64]{3,2,1,0:T(8,128)(2,1)S(1)} %fusion.26) | data formatting | bytes 2097152 | tf_op jit(solution)/shard_map/dot_general | solution.py:67
  5.5 1.6 %fusion.3 = f32[64,2,1024]{2,0,1:T(8,128)S(1)} fusion(s16[1024]{0:T(1024)(128)(2,1)S(1)} %get-tuple-element.5, bf16[64,2,4096]{2,1,0:T(2,128)(2,1)S(1)} %dot_general.22), kind=kOutput, calls=%fused_computation.6 | convolution fusion | flops 1082130432 | bytes 1574912 | tf_op jit(solution)/shard_map/dot_general | solution.py:67
  7.2 1.6 %fusion.5 = f32[64,2,1024]{2,0,1:T(8,128)S(1)} fusion(s16[1024]{0:T(1024)(128)(2,1)S(1)} %get-tuple-element.6, bf16[64,2,4096]{2,1,0:T(2,128)(2,1)S(1)} %dot_general.22), kind=kOutput, calls=%fused_computation.7 | convolution fusion | flops 1082130432 | bytes 1574912 | tf_op jit(solution)/shard_map/dot_general | solution.py:67
  8.8 1.6 %fusion.7 = f32[64,2,1024]{2,0,1:T(8,128)S(1)} fusion(s16[1024]{0:T(1024)(128)(2,1)S(1)} %get-tuple-element.7, bf16[64,2,4096]{2,1,0:T(2,128)(2,1)S(1)} %dot_general.22), kind=kOutput, calls=%fused_computation.8 | convolution fusion | flops 1082130432 | bytes 1574912 | tf_op jit(solution)/shard_map/dot_general | solution.py:67
  10.4 0.0 copy-start.1
  10.5 0.0 copy-start.2
  10.5 0.1 fusion.36
  10.6 0.1 fusion.37
  10.8 0.3 copy-done.1
  11.1 0.0 copy-done.2
  11.1 0.1 pad_maximum_fusion.1
  11.2 12.2 %all_to_all.10 = bf16[8,2,72,128]{3,2,1,0:T(8,128)(2,1)S(1)} all-to-all(bf16[8,2,72,128]{3,2,1,0:T(8,128)(2,1)S(1)} %pad_maximum_fusion), channel_id=1, replica_groups=mesh['sub'=64,'grp'=8] {'grp'}, dimensions={0} | all-to-all | bytes 589824 | tf_op jit(solution)/shard_map/all_to_all | solution.py:80
  23.4 0.1 slice_add_fusion
  23.5 0.5 fusion.28
  24.1 39.5 %all_to_all.11 = bf16[64,8,2,128]{3,1,2,0:T(8,128)(2,1)S(1)} all-to-all(bf16[64,8,2,128]{3,1,2,0:T(8,128)(2,1)S(1)} %copy.16), channel_id=1, replica_groups=mesh['sub'=64,'grp'=8] {'sub'}, dimensions={0} | all-to-all | bytes 524288 | tf_op jit(solution)/shard_map/all_to_all | solution.py:92
  63.6 0.1 convert_reduce_fusion
  63.6 0.6 copy.18
  (16 shorter events, 0.3 us)
Async XLA Ops:
  3.9 1.5 %copy-start = (s32[3,1024]{1,0:T(4,128)S(1)}, s32[3,1024]{1,0:T(4,128)}, u32[]{:S(2)}) copy-start(s32[3,1024]{1,0:T(4,128)} %param.7) | copy-start | bytes 36868
  10.4 0.7 %copy-start.1 = (s32[1,64]{1,0:T(1,128)S(1)}, s32[1,64]{1,0:T(1,128)}, u32[]{:S(2)}) copy-start(s32[1,64]{1,0:T(1,128)} %param.6) | copy-start | bytes 772
  10.5 0.7 %copy-start.2 = (s32[1,64]{1,0:T(1,128)S(1)}, s32[1,64]{1,0:T(1,128)}, u32[]{:S(2)}) copy-start(s32[1,64]{1,0:T(1,128)} %param.5) | copy-start | bytes 772

commit v9 on v8

--- a/solution.py
+++ b/solution.py
@@ -45,7 +45,7 @@
     spec = jnp.einsum(
         "pjqi,niqk->npkj", rotation_tables(right), halves, preferred_element_type=jnp.float32
     ).astype(jnp.bfloat16)
-    return spec.reshape(count * 2, box * box)
+    return spec.reshape(count * 2, box, box)
 
 
 def local(tiles, dest_owner, dest_slot, triples):
@@ -56,15 +56,16 @@
     peers = lax.axis_size("sub")
     right, left, window = make_tables(patch, BOX)
     spec = spectra_tile_major(frames, right, window)
-    freq_ids = jnp.arange(spec.shape[1], dtype=jnp.int16)[:, None]
+    axis_ids = jnp.arange(BOX, dtype=jnp.int16)
+    freq_ids = (axis_ids[:, None] * BOX + axis_ids[None, :])[:, :, None]
     one = jnp.ones((), jnp.bfloat16)
     zero = jnp.zeros((), jnp.bfloat16)
     picked = []
     swapped = (triples % BOX) * BOX + triples // BOX
     for which in range(3):
-        hit = freq_ids == swapped[which].astype(jnp.int16)[None, :]
+        hit = freq_ids == swapped[which].astype(jnp.int16)[None, None, :]
         select = jnp.where(hit, one, zero)
-        picked.append(jnp.dot(spec, select, preferred_element_type=jnp.float32))
+        picked.append(jnp.einsum("rkj,kjt->rt", spec, select, preferred_element_type=jnp.float32))
     ntri = triples.shape[1]
     first, second, third = [p.reshape(count, 2, ntri) for p in picked]
     prod_real = first[:, 0] * second[:, 0] - first[:, 1] * second[:, 1]

time: 64.5 us -> 72 us (1.12)
  matrix products: 8.5 us -> 14.6 us
  local copies, waits for them, and re-layouts: 2.6 us -> 4.03 us
    dot_general x3, matrix products: 4.91 us -> 11 us  [local(): jnp.einsum('rkj,kjt->rt', spec, select, preferred_element_type=jnp.float32)]
    dot_general x1, local copies, waits for them, and re-layouts: 1.5 us -> 2.93 us  [local(): jnp.einsum('rkj,kjt->rt', spec, select, preferred_element_type=jnp.float32)]
where the time goes in v9:
time: 72 us; the launch traced here: 71.8 us
  blocking collectives  51.7 us (72%)
  matrix products  14.6 us (20%)
  local copies, waits for them, and re-layouts  4.03 us (6%)
  other arithmetic  1.32 us (2%)
    all_to_all x1, blocking collectives, local(): lax.all_to_all(shaped, 'sub', split_axis=0, concat_axis=0, tiled=True)  39.5 us
    all_to_all x1, blocking collectives, local(): lax.all_to_all(payload, 'grp', split_axis=0, concat_axis=0, tiled=True)  12.2 us
    dot_general x3, matrix products, local(): jnp.einsum('rkj,kjt->rt', spec, select, preferred_element_type=jnp.float32)  11 us
    dot_general x1, local copies, waits for them, and re-layouts, local(): jnp.einsum('rkj,kjt->rt', spec, select, preferred_element_type=jnp.float32)  2.93 us
    dot_general x1, matrix products, spectra_tile_major(): jnp.einsum('nij,jc->nic', apodised, right, preferred_element_type=jnp.flo...  2.32 us

profile of v9, /device:TPU:6, one launch (start us, length us, event | category | flops | bytes accessed | tf_op | source)
XLA Modules:
  0.0 71.8 jit_solution(5630871506784274326)
XLA Ops:
  0.0 0.2 multiply_convert_fusion
  0.2 0.2 fusion.68
  0.4 0.2 multiply_convert_fusion.3
  0.7 0.1 broadcast_multiply_fusion
  0.8 2.3 %fusion.26 = bf16[64,128,128]{1,2,0:T(8,128)(2,1)S(1)} fusion(bf16[1,64,128,128]{3,2,1,0:T(8,128)(2,1)} %param.4, f32[128,128]{1,0:T(8,128)S(1)} %broadcast_multiply_fusion, bf16[128,64]{0,1:T(8,128)(2,1)S(1)} %get-tuple-element.16, bf16[128,64]{0,1:T(8,128)(2,1)S(1)} %get-tuple-element.15), kind=kOutput, calls=%fused_computation.27 | convolution fusion | flops 272695296 | bytes 4292608 | tf_op jit(solution)/shard_map/nij,jc->nic/dot_general | solution.py:41
  3.2 0.7 fusion.29
  3.9 0.0 copy-start.1
  3.9 2.9 %copy.14 = bf16[64,2,64,64]{3,0,2,1:T(8,128)(2,1)} copy(bf16[64,2,64,64]{2,3,1,0:T(8,128)(2,1)S(1)} %fusion.29) | data formatting | bytes 2097152 | tf_op jit(solution)/shard_map/rkj,kjt->rt/dot_general | solution.py:68
  6.9 4.8 %fusion.36 = f32[64,2,1024]{2,0,1:T(8,128)S(1)} fusion(bf16[64,2,64,64]{3,0,2,1:T(8,128)(2,1)} %copy.14, s16[1024]{0:T(1024)(128)(2,1)S(1)} %get-tuple-element.5, s16[64,64]{0,1:T(8,128)(2,1)S(1)} %iota_add_fusion), kind=kOutput, calls=%fused_computation.31 | convolution fusion | flops 1082130432 | bytes 1583104 | tf_op jit(solution)/shard_map/rkj,kjt->rt/dot_general | solution.py:68
  11.8 3.1 %fusion.30 = f32[64,2,1024]{2,0,1:T(8,128)S(1)} fusion(bf16[64,2,64,64]{3,0,2,1:T(8,128)(2,1)S(1)} %copy-done, s16[1024]{0:T(1024)(128)(2,1)S(1)} %get-tuple-element.7, s16[64,64]{0,1:T(8,128)(2,1)S(1)} %iota_add_fusion), kind=kOutput, calls=%fused_computation.29 | convolution fusion | flops 1082130432 | bytes 1583104 | tf_op jit(solution)/shard_map/rkj,kjt->rt/dot_general | solution.py:68
  14.9 3.1 %fusion.33 = f32[64,2,1024]{2,0,1:T(8,128)S(1)} fusion(bf16[64,2,64,64]{3,0,2,1:T(8,128)(2,1)S(1)} %copy-done, s16[1024]{0:T(1024)(128)(2,1)S(1)} %get-tuple-element.6, s16[64,64]{0,1:T(8,128)(2,1)S(1)} %iota_add_fusion), kind=kOutput, calls=%fused_computation.30 | convolution fusion | flops 1082130432 | bytes 1583104 | tf_op jit(solution)/shard_map/rkj,kjt->rt/dot_general | solution.py:68
  18.0 0.0 copy-start.2
  18.0 0.0 copy-start.3
  18.0 0.1 fusion.45
  18.2 0.1 fusion.46
  18.4 0.3 copy-done.2
  18.7 0.0 copy-done.3
  18.7 0.1 pad_maximum_fusion.1
  18.8 12.2 %all_to_all.10 = bf16[8,2,72,128]{3,2,1,0:T(8,128)(2,1)S(1)} all-to-all(bf16[8,2,72,128]{3,2,1,0:T(8,128)(2,1)S(1)} %pad_maximum_fusion), channel_id=1, replica_groups=mesh['sub'=64,'grp'=8] {'grp'}, dimensions={0} | all-to-all | bytes 589824 | tf_op jit(solution)/shard_map/all_to_all | solution.py:81
  31.0 0.1 slice_add_fusion
  31.0 0.5 fusion.40
  31.7 39.5 %all_to_all.11 = bf16[64,8,2,128]{3,1,2,0:T(8,128)(2,1)S(1)} all-to-all(bf16[64,8,2,128]{3,1,2,0:T(8,128)(2,1)S(1)} %copy.20), channel_id=1, replica_groups=mesh['sub'=64,'grp'=8] {'sub'}, dimensions={0} | all-to-all | bytes 524288 | tf_op jit(solution)/shard_map/all_to_all | solution.py:93
  71.2 0.1 convert_reduce_fusion
  71.2 0.6 copy.22
  (20 shorter events, 0.4 us)
Async XLA Ops:
  3.9 3.0 %copy-start.1 = (s32[3,1024]{1,0:T(4,128)S(1)}, s32[3,1024]{1,0:T(4,128)}, u32[]{:S(2)}) copy-start(s32[3,1024]{1,0:T(4,128)} %param.7) | copy-start | bytes 36868
  6.9 4.8 %copy-start = (bf16[64,2,64,64]{3,0,2,1:T(8,128)(2,1)S(1)}, bf16[64,2,64,64]{3,0,2,1:T(8,128)(2,1)}, u32[]{:S(2)}) copy-start(bf16[64,2,64,64]{3,0,2,1:T(8,128)(2,1)} %copy.14) | copy-start | bytes 3145732
  18.0 0.7 copy-start.2
  18.0 0.7 copy-start.3

commit v10 on v8

--- a/solution.py
+++ b/solution.py
@@ -73,13 +73,13 @@
     out_imag = prod_imag * third[:, 0] - prod_real * third[:, 1]
     terms = jnp.stack([out_real, out_imag], axis=0).astype(jnp.bfloat16)
     block = ntri // groups
-    terms = jnp.transpose(terms.reshape(2, count, groups, block), (2, 0, 1, 3))
+    terms = jnp.transpose(terms.reshape(2 * count, groups, block), (1, 0, 2))
     label = jnp.concatenate([dest_owner[0], dest_slot[0]]).astype(jnp.bfloat16)
-    marks = jnp.broadcast_to(label[None, None, None, :], (groups, 2, 8, 2 * count))
-    payload = jnp.concatenate([terms, marks], axis=2)
+    marks = jnp.broadcast_to(label[None, None, :], (groups, 8, 2 * count))
+    payload = jnp.concatenate([terms, marks], axis=1)
     got = lax.all_to_all(payload, "grp", split_axis=0, concat_axis=0, tiled=True)
-    got_terms = got[:, :, :count]
-    got_label = got[:, 0, count].astype(jnp.int32)
+    got_terms = got[:, : 2 * count].reshape(groups, 2, count, block)
+    got_label = got[:, 2 * count].astype(jnp.int32)
     got_marks = got_label[:, :count] * OWN + got_label[:, count:]
     rows = peers * OWN
     onehot = (

time: 64.5 us -> 64.4 us (level)
  no operation moved by 1% of the time
where the time goes in v10:
time: 64.4 us; the launch traced here: 64.2 us
  blocking collectives  51.6 us (80%)
  matrix products  8.5 us (13%)
  local copies, waits for them, and re-layouts  2.63 us (4%)
  other arithmetic  1.31 us (2%)
    all_to_all x1, blocking collectives, local(): lax.all_to_all(shaped, 'sub', split_axis=0, concat_axis=0, tiled=True)  39.6 us
    all_to_all x1, blocking collectives, local(): lax.all_to_all(payload, 'grp', split_axis=0, concat_axis=0, tiled=True)  12 us
    dot_general x3, matrix products, local(): picked.append(jnp.dot(spec, select, preferred_element_type=jnp.float32))  4.91 us
    dot_general x1, matrix products, spectra_tile_major(): jnp.einsum('nij,jc->nic', apodised, right, preferred_element_type=jnp.flo...  2.32 us
    dot_general x1, local copies, waits for them, and re-layouts, local(): picked.append(jnp.dot(spec, select, preferred_element_type=jnp.float32))  1.5 us

profile of v10, /device:TPU:6, one launch (start us, length us, event | category | flops | bytes accessed | tf_op | source)
XLA Modules:
  0.0 64.2 jit_solution(16875446204921928907)
XLA Ops:
  0.0 0.2 multiply_convert_fusion
  0.2 0.2 fusion.58
  0.4 0.2 multiply_convert_fusion.3
  0.7 0.1 broadcast_multiply_fusion
  0.8 2.3 %fusion.23 = bf16[64,128,128]{1,2,0:T(8,128)(2,1)S(1)} fusion(bf16[1,64,128,128]{3,2,1,0:T(8,128)(2,1)} %param.4, f32[128,128]{1,0:T(8,128)S(1)} %broadcast_multiply_fusion, bf16[128,64]{0,1:T(8,128)(2,1)S(1)} %get-tuple-element.16, bf16[128,64]{0,1:T(8,128)(2,1)S(1)} %get-tuple-element.15), kind=kOutput, calls=%fused_computation.24 | convolution fusion | flops 272695296 | bytes 4292608 | tf_op jit(solution)/shard_map/nij,jc->nic/dot_general | solution.py:41
  3.2 0.7 %fusion.26 = bf16[64,2,64,64]{3,2,1,0:T(8,128)(2,1)S(1)} fusion(bf16[64,128,2,64,1]{1,3,2,4,0:T(8,128)(2,1)S(1)} %bitcast.75, bf16[1,64,2,128]{3,1,2,0:T(8,128)(2,1)S(1)} %get-tuple-element.12, bf16[1,64,2,128]{3,1,2,0:T(8,128)(2,1)S(1)} %get-tuple-element.11), kind=kOutput, calls=%fused_computation.25 | convolution fusion | flops 269090816 | bytes 3211264 | tf_op jit(solution)/shard_map/pjqi,niqk->npkj/dot_general | solution.py:45
  3.9 0.0 copy-start
  3.9 1.5 %dot_general.22 = bf16[64,2,4096]{2,1,0:T(2,128)(2,1)S(1)} reshape(bf16[64,2,64,64]{3,2,1,0:T(8,128)(2,1)S(1)} %fusion.26) | data formatting | bytes 2097152 | tf_op jit(solution)/shard_map/dot_general | solution.py:67
  5.5 1.6 %fusion.3 = f32[64,2,1024]{2,0,1:T(8,128)S(1)} fusion(s16[1024]{0:T(1024)(128)(2,1)S(1)} %get-tuple-element.5, bf16[64,2,4096]{2,1,0:T(2,128)(2,1)S(1)} %dot_general.22), kind=kOutput, calls=%fused_computation.6 | convolution fusion | flops 1082130432 | bytes 1574912 | tf_op jit(solution)/shard_map/dot_general | solution.py:67
  7.2 1.6 %fusion.5 = f32[64,2,1024]{2,0,1:T(8,128)S(1)} fusion(s16[1024]{0:T(1024)(128)(2,1)S(1)} %get-tuple-element.6, bf16[64,2,4096]{2,1,0:T(2,128)(2,1)S(1)} %dot_general.22), kind=kOutput, calls=%fused_computation.7 | convolution fusion | flops 1082130432 | bytes 1574912 | tf_op jit(solution)/shard_map/dot_general | solution.py:67
  8.8 1.6 %fusion.7 = f32[64,2,1024]{2,0,1:T(8,128)S(1)} fusion(s16[1024]{0:T(1024)(128)(2,1)S(1)} %get-tuple-element.7, bf16[64,2,4096]{2,1,0:T(2,128)(2,1)S(1)} %dot_general.22), kind=kOutput, calls=%fused_computation.8 | convolution fusion | flops 1082130432 | bytes 1574912 | tf_op jit(solution)/shard_map/dot_general | solution.py:67
  10.4 0.0 copy-start.1
  10.5 0.0 copy-start.2
  10.5 0.1 fusion.35
  10.6 0.1 fusion.36
  10.8 0.3 copy-done.1
  11.1 0.0 copy-done.2
  11.1 0.1 pad_maximum_fusion.2
  11.2 12.0 %all_to_all.10 = bf16[8,136,128]{2,1,0:T(8,128)(2,1)S(1)} all-to-all(bf16[8,136,128]{2,1,0:T(8,128)(2,1)S(1)} %pad_maximum_fusion), channel_id=1, replica_groups=mesh['sub'=64,'grp'=8] {'grp'}, dimensions={0} | all-to-all | bytes 557056 | tf_op jit(solution)/shard_map/all_to_all | solution.py:80
  23.2 0.1 slice_add_fusion
  23.3 0.5 fusion.28
  23.9 39.6 %all_to_all.11 = bf16[64,8,2,128]{3,1,2,0:T(8,128)(2,1)S(1)} all-to-all(bf16[64,8,2,128]{3,1,2,0:T(8,128)(2,1)S(1)} %copy.18), channel_id=1, replica_groups=mesh['sub'=64,'grp'=8] {'sub'}, dimensions={0} | all-to-all | bytes 524288 | tf_op jit(solution)/shard_map/all_to_all | solution.py:92
  63.5 0.1 convert_reduce_fusion
  63.6 0.6 copy.20
  (15 shorter events, 0.4 us)
Async XLA Ops:
  3.9 1.5 %copy-start = (s32[3,1024]{1,0:T(4,128)S(1)}, s32[3,1024]{1,0:T(4,128)}, u32[]{:S(2)}) copy-start(s32[3,1024]{1,0:T(4,128)} %param.7) | copy-start | bytes 36868
  10.4 0.7 %copy-start.1 = (s32[1,64]{1,0:T(1,128)S(1)}, s32[1,64]{1,0:T(1,128)}, u32[]{:S(2)}) copy-start(s32[1,64]{1,0:T(1,128)} %param.6) | copy-start | bytes 772
  10.5 0.7 %copy-start.2 = (s32[1,64]{1,0:T(1,128)S(1)}, s32[1,64]{1,0:T(1,128)}, u32[]{:S(2)}) copy-start(s32[1,64]{1,0:T(1,128)} %param.5) | copy-start | bytes 772

commit v11 on v8

--- a/solution.py
+++ b/solution.py
@@ -59,13 +59,12 @@
     freq_ids = jnp.arange(spec.shape[1], dtype=jnp.int16)[:, None]
     one = jnp.ones((), jnp.bfloat16)
     zero = jnp.zeros((), jnp.bfloat16)
-    picked = []
     swapped = (triples % BOX) * BOX + triples // BOX
-    for which in range(3):
-        hit = freq_ids == swapped[which].astype(jnp.int16)[None, :]
-        select = jnp.where(hit, one, zero)
-        picked.append(jnp.dot(spec, select, preferred_element_type=jnp.float32))
+    hit = freq_ids == swapped.reshape(1, -1).astype(jnp.int16)
+    select = jnp.where(hit, one, zero)
+    every = jnp.dot(spec, select, preferred_element_type=jnp.float32)
     ntri = triples.shape[1]
+    picked = [every[:, which * ntri : (which + 1) * ntri] for which in range(3)]
     first, second, third = [p.reshape(count, 2, ntri) for p in picked]
     prod_real = first[:, 0] * second[:, 0] - first[:, 1] * second[:, 1]
     prod_imag = first[:, 0] * second[:, 1] + first[:, 1] * second[:, 0]

time: 64.5 us -> 65.7 us (1.019)
  local copies, waits for them, and re-layouts: 2.6 us -> 4.78 us
  matrix products: 8.5 us -> 7.25 us
    reshape x0 -> x4, local copies, waits for them, and re-layouts: none -> 2.59 us  [the longest x1 1.68 us: spectra_tile_major(): return spec.reshape(count * 2, box * box)]
    dot_general x1 -> x0, local copies, waits for them, and re-layouts: 1.5 us -> none  [local(): picked.append(jnp.dot(spec, select, preferred_element_type=jnp.float32))]
    slice x1 -> x3, local copies, waits for them, and re-layouts: 0.05 us -> 1.32 us  [the longest x1 0.81 us: local(): prod_real = first[:, 0] * second[:, 0] - first[:, 1] * second[:, 1]]
    dot_general x3 -> x1, matrix products: 4.91 us -> 3.66 us  [local(): every = jnp.dot(spec, select, preferred_element_type=jnp.float32)]
where the time goes in v11:
time: 65.7 us; the launch traced here: 65.5 us
  blocking collectives  51.6 us (79%)
  matrix products  7.25 us (11%)
  local copies, waits for them, and re-layouts  4.78 us (7%)
  other arithmetic  1.58 us (2%)
    all_to_all x1, blocking collectives, local(): lax.all_to_all(shaped, 'sub', split_axis=0, concat_axis=0, tiled=True)  39.5 us
    all_to_all x1, blocking collectives, local(): lax.all_to_all(payload, 'grp', split_axis=0, concat_axis=0, tiled=True)  12.2 us
    dot_general x1, matrix products, local(): every = jnp.dot(spec, select, preferred_element_type=jnp.float32)  3.66 us
    dot_general x1, matrix products, spectra_tile_major(): jnp.einsum('nij,jc->nic', apodised, right, preferred_element_type=jnp.flo...  2.32 us
    reshape x1, local copies, waits for them, and re-layouts, spectra_tile_major(): return spec.reshape(count * 2, box * box)  1.68 us

profile of v11, /device:TPU:6, one launch (start us, length us, event | category | flops | bytes accessed | tf_op | source)
XLA Modules:
  0.0 65.5 jit_solution(1325381658513964743)
XLA Ops:
  0.0 0.2 multiply_convert_fusion
  0.2 0.2 fusion.43
  0.4 0.2 multiply_convert_fusion.3
  0.7 0.1 broadcast_multiply_fusion
  0.8 2.3 %fusion.10 = bf16[64,128,128]{1,2,0:T(8,128)(2,1)S(1)} fusion(bf16[1,64,128,128]{3,2,1,0:T(8,128)(2,1)} %param.4, f32[128,128]{1,0:T(8,128)S(1)} %broadcast_multiply_fusion, bf16[128,64]{0,1:T(8,128)(2,1)S(1)} %get-tuple-element.22, bf16[128,64]{0,1:T(8,128)(2,1)S(1)} %get-tuple-element.21), kind=kOutput, calls=%fused_computation.12 | convolution fusion | flops 272695296 | bytes 4292608 | tf_op jit(solution)/shard_map/nij,jc->nic/dot_general | solution.py:41
  3.2 0.7 %fusion.13 = bf16[64,2,64,64]{3,2,1,0:T(8,128)(2,1)S(1)} fusion(bf16[64,128,2,64,1]{1,3,2,4,0:T(8,128)(2,1)S(1)} %bitcast.69, bf16[1,64,2,128]{3,1,2,0:T(8,128)(2,1)S(1)} %get-tuple-element.18, bf16[1,64,2,128]{3,1,2,0:T(8,128)(2,1)S(1)} %get-tuple-element.17), kind=kOutput, calls=%fused_computation.13 | convolution fusion | flops 269090816 | bytes 3211264 | tf_op jit(solution)/shard_map/pjqi,niqk->npkj/dot_general | solution.py:45
  3.9 1.7 %reshape.417 = bf16[128,4096]{1,0:T(8,128)(2,1)S(1)} reshape(bf16[64,2,64,64]{3,2,1,0:T(8,128)(2,1)S(1)} %fusion.13) | data formatting | bytes 2097152 | tf_op jit(solution)/shard_map/reshape | solution.py:48
  5.7 3.7 %fusion = f32[128,3072]{1,0:T(8,128)S(1)} fusion(bf16[128,4096]{1,0:T(8,128)(2,1)S(1)} %reshape.417, s16[3072]{0:T(1024)(128)(2,1)S(1)} %convert_element_type.126), kind=kOutput, calls=%fused_computation.1 | convolution fusion | flops 3246391296 | bytes 2627584 | tf_op jit(solution)/shard_map/dot_general | solution.py:65
  9.3 0.1 fusion.48
  9.4 0.3 reshape.418
  9.7 0.3 reshape.419
  10.1 0.3 reshape.420
  10.4 0.4 fusion.51
  10.8 0.8 %fusion.49 = (f32[64,1,1024]{2,1,0:T(1,128)S(1)}, f32[64,1,1024]{2,1,0:T(1,128)S(1)}, f32[64,1,1024]{2,1,0:T(1,128)S(1)}, f32[64,1,1024]{2,1,0:T(1,128)S(1)}) fusion(f32[64,2,1024]{2,1,0:T(2,128)S(1)} %reshape.418, f32[64,2,1024]{2,1,0:T(2,128)S(1)} %reshape.419), kind=kLoop, calls=%fused_computation.85 | loop fusion | bytes 2097152 | tf_op jit(solution)/shard_map/slice | solution.py:69
  11.6 0.3 fusion.20
  12.0 0.1 fusion.21
  12.2 0.1 copy-done.1
  12.3 0.1 pad_maximum_fusion.1
  12.5 12.2 %all_to_all.10 = bf16[8,2,72,128]{3,2,1,0:T(8,128)(2,1)S(1)} all-to-all(bf16[8,2,72,128]{3,2,1,0:T(8,128)(2,1)S(1)} %copy.19), channel_id=1, replica_groups=mesh['sub'=64,'grp'=8] {'grp'}, dimensions={0} | all-to-all | bytes 589824 | tf_op jit(solution)/shard_map/all_to_all | solution.py:79
  24.6 0.1 slice_add_fusion
  24.7 0.5 fusion.15
  25.3 39.5 %all_to_all.11 = bf16[64,8,2,128]{3,1,2,0:T(8,128)(2,1)S(1)} all-to-all(bf16[64,8,2,128]{3,1,2,0:T(8,128)(2,1)S(1)} %copy.21), channel_id=1, replica_groups=mesh['sub'=64,'grp'=8] {'sub'}, dimensions={0} | all-to-all | bytes 524288 | tf_op jit(solution)/shard_map/all_to_all | solution.py:91
  64.8 0.1 convert_reduce_fusion
  64.9 0.6 copy.23
  (19 shorter events, 0.4 us)
Async XLA Ops:
  3.9 1.7 %copy-start = (s32[3,1024]{1,0:T(4,128)S(1)}, s32[3,1024]{1,0:T(4,128)}, u32[]{:S(2)}) copy-start(s32[3,1024]{1,0:T(4,128)} %param.7) | copy-start | bytes 36868
  11.6 0.7 %copy-start.1 = (s32[1,64]{1,0:T(1,128)S(1)}, s32[1,64]{1,0:T(1,128)}, u32[]{:S(2)}) copy-start(s32[1,64]{1,0:T(1,128)} %param.6) | copy-start | bytes 772
  11.6 0.7 %copy-start.2 = (s32[1,64]{1,0:T(1,128)S(1)}, s32[1,64]{1,0:T(1,128)}, u32[]{:S(2)}) copy-start(s32[1,64]{1,0:T(1,128)} %param.5) | copy-start | bytes 772

commit v12 on v8

--- a/solution.py
+++ b/solution.py
@@ -82,9 +82,8 @@
     got_label = got[:, 0, count].astype(jnp.int32)
     got_marks = got_label[:, :count] * OWN + got_label[:, count:]
     rows = peers * OWN
-    onehot = (
-        got_marks[None, :, :] == jnp.arange(rows, dtype=jnp.int32)[:, None, None]
-    ).astype(jnp.bfloat16)
+    row_ids = jnp.arange(rows, dtype=jnp.int16)[:, None, None]
+    onehot = jnp.where(got_marks.astype(jnp.int16)[None, :, :] == row_ids, one, zero)
     partial_value = jnp.einsum(
         "rgn,gcnt->rct", onehot, got_terms, preferred_element_type=jnp.float32
     )

time: 64.5 us -> 64.4 us (level)
  no operation moved by 1% of the time
where the time goes in v12:
time: 64.4 us; the launch traced here: 64.2 us
  blocking collectives  51.6 us (80%)
  matrix products  8.42 us (13%)
  local copies, waits for them, and re-layouts  2.6 us (4%)
  other arithmetic  1.31 us (2%)
    all_to_all x1, blocking collectives, local(): lax.all_to_all(shaped, 'sub', split_axis=0, concat_axis=0, tiled=True)  39.5 us
    all_to_all x1, blocking collectives, local(): lax.all_to_all(payload, 'grp', split_axis=0, concat_axis=0, tiled=True)  12.2 us
    dot_general x3, matrix products, local(): picked.append(jnp.dot(spec, select, preferred_element_type=jnp.float32))  4.91 us
    dot_general x1, matrix products, spectra_tile_major(): jnp.einsum('nij,jc->nic', apodised, right, preferred_element_type=jnp.flo...  2.32 us
    dot_general x1, local copies, waits for them, and re-layouts, local(): picked.append(jnp.dot(spec, select, preferred_element_type=jnp.float32))  1.5 us

profile of v12, /device:TPU:6, one launch (start us, length us, event | category | flops | bytes accessed | tf_op | source)
XLA Modules:
  0.0 64.2 jit_solution(13576452462998969580)
XLA Ops:
  0.0 0.2 multiply_convert_fusion
  0.2 0.2 fusion.62
  0.4 0.2 multiply_convert_fusion.3
  0.7 0.1 broadcast_multiply_fusion
  0.8 2.3 %fusion.23 = bf16[64,128,128]{1,2,0:T(8,128)(2,1)S(1)} fusion(bf16[1,64,128,128]{3,2,1,0:T(8,128)(2,1)} %param.4, f32[128,128]{1,0:T(8,128)S(1)} %broadcast_multiply_fusion, bf16[128,64]{0,1:T(8,128)(2,1)S(1)} %get-tuple-element.16, bf16[128,64]{0,1:T(8,128)(2,1)S(1)} %get-tuple-element.15), kind=kOutput, calls=%fused_computation.24 | convolution fusion | flops 272695296 | bytes 4292608 | tf_op jit(solution)/shard_map/nij,jc->nic/dot_general | solution.py:41
  3.2 0.7 %fusion.26 = bf16[64,2,64,64]{3,2,1,0:T(8,128)(2,1)S(1)} fusion(bf16[64,128,2,64,1]{1,3,2,4,0:T(8,128)(2,1)S(1)} %bitcast.77, bf16[1,64,2,128]{3,1,2,0:T(8,128)(2,1)S(1)} %get-tuple-element.12, bf16[1,64,2,128]{3,1,2,0:T(8,128)(2,1)S(1)} %get-tuple-element.11), kind=kOutput, calls=%fused_computation.25 | convolution fusion | flops 269090816 | bytes 3211264 | tf_op jit(solution)/shard_map/pjqi,niqk->npkj/dot_general | solution.py:45
  3.9 0.0 copy-start
  3.9 1.5 %dot_general.22 = bf16[64,2,4096]{2,1,0:T(2,128)(2,1)S(1)} reshape(bf16[64,2,64,64]{3,2,1,0:T(8,128)(2,1)S(1)} %fusion.26) | data formatting | bytes 2097152 | tf_op jit(solution)/shard_map/dot_general | solution.py:67
  5.5 1.6 %fusion.3 = f32[64,2,1024]{2,0,1:T(8,128)S(1)} fusion(s16[1024]{0:T(1024)(128)(2,1)S(1)} %get-tuple-element.5, bf16[64,2,4096]{2,1,0:T(2,128)(2,1)S(1)} %dot_general.22), kind=kOutput, calls=%fused_computation.6 | convolution fusion | flops 1082130432 | bytes 1574912 | tf_op jit(solution)/shard_map/dot_general | solution.py:67
  7.2 1.6 %fusion.5 = f32[64,2,1024]{2,0,1:T(8,128)S(1)} fusion(s16[1024]{0:T(1024)(128)(2,1)S(1)} %get-tuple-element.6, bf16[64,2,4096]{2,1,0:T(2,128)(2,1)S(1)} %dot_general.22), kind=kOutput, calls=%fused_computation.7 | convolution fusion | flops 1082130432 | bytes 1574912 | tf_op jit(solution)/shard_map/dot_general | solution.py:67
  8.8 1.6 %fusion.7 = f32[64,2,1024]{2,0,1:T(8,128)S(1)} fusion(s16[1024]{0:T(1024)(128)(2,1)S(1)} %get-tuple-element.7, bf16[64,2,4096]{2,1,0:T(2,128)(2,1)S(1)} %dot_general.22), kind=kOutput, calls=%fused_computation.8 | convolution fusion | flops 1082130432 | bytes 1574912 | tf_op jit(solution)/shard_map/dot_general | solution.py:67
  10.4 0.0 copy-start.1
  10.5 0.0 copy-start.2
  10.5 0.1 fusion.39
  10.6 0.1 fusion.40
  10.8 0.3 copy-done.1
  11.1 0.0 copy-done.2
  11.1 0.1 pad_maximum_fusion.1
  11.2 12.2 %all_to_all.10 = bf16[8,2,72,128]{3,2,1,0:T(8,128)(2,1)S(1)} all-to-all(bf16[8,2,72,128]{3,2,1,0:T(8,128)(2,1)S(1)} %pad_maximum_fusion), channel_id=1, replica_groups=mesh['sub'=64,'grp'=8] {'grp'}, dimensions={0} | all-to-all | bytes 589824 | tf_op jit(solution)/shard_map/all_to_all | solution.py:80
  23.4 0.1 add_convert_fusion.1
  23.5 0.5 fusion.28
  24.0 39.5 %all_to_all.11 = bf16[64,8,2,128]{3,1,2,0:T(8,128)(2,1)S(1)} all-to-all(bf16[64,8,2,128]{3,1,2,0:T(8,128)(2,1)S(1)} %copy.16), channel_id=1, replica_groups=mesh['sub'=64,'grp'=8] {'sub'}, dimensions={0} | all-to-all | bytes 524288 | tf_op jit(solution)/shard_map/all_to_all | solution.py:91
  63.5 0.1 convert_reduce_fusion
  63.6 0.6 copy.18
  (16 shorter events, 0.3 us)
Async XLA Ops:
  3.9 1.5 %copy-start = (s32[3,1024]{1,0:T(4,128)S(1)}, s32[3,1024]{1,0:T(4,128)}, u32[]{:S(2)}) copy-start(s32[3,1024]{1,0:T(4,128)} %param.7) | copy-start | bytes 36868
  10.4 0.7 %copy-start.1 = (s32[1,64]{1,0:T(1,128)S(1)}, s32[1,64]{1,0:T(1,128)}, u32[]{:S(2)}) copy-start(s32[1,64]{1,0:T(1,128)} %param.6) | copy-start | bytes 772
  10.5 0.7 %copy-start.2 = (s32[1,64]{1,0:T(1,128)S(1)}, s32[1,64]{1,0:T(1,128)}, u32[]{:S(2)}) copy-start(s32[1,64]{1,0:T(1,128)} %param.5) | copy-start | bytes 772
